TPU v7x, 256 devices: a whole 4x4x8 slice. The times are simulated.
256 devices in a mesh: query: 8 (over x, core), bank: 32 (over z, y).
Axes of the slice: x: 4, y: 4, z: 8, core: 2. Of those that a mesh axis runs over, the one named last changes fastest.
Arguments:
- queries: bfloat16 [2048, 32, 128], P(('query', 'bank'))
- passages: bfloat16 [8192, 128, 128], P('bank')
- passage_home: int32 [8192], replicated, may hold values from 0 to 8191, as said below
- candidates: int32 [2048, 16], P(('query', 'bank')), may hold values from 0 to 8191, as said below
- positive: int32 [2048], P(('query', 'bank')), may hold values from 0 to 15
Outputs:
- losses: float32 [2048], P(('query', 'bank'))
- query_grads: float32 [2048, 32, 128], P(('query', 'bank'))
Inputs may be any that keep to these rules, and one draw needn't show every extreme that they name: `passage_home`: each passage id has its own storage row; storage row r lies on bank index r // 256. `candidates`: among the 128 list entries of one device's queries (aligned blocks of 8 queries, in order), at most 12 name passages stored on one bank index; in every block some bank index gets exactly 12, and in each group of 32 consecutive blocks it is the same bank index for all of them.
All inputs are finite; a program needn't handle non-finite values.
Results may differ from a plain program's by a relative error of at most 0.0049.
Values may be sent and summed in bfloat16 or wider, within the bound.
No kernel may reach another device: no remote copies, remote signals or barrier semaphores. Data moves between devices by JAX's collectives and lax.ppermute only.
A program may use at most 128 MiB of HBM per device.

v0:
```python
import jax
import jax.numpy as jnp
from jax import lax
from jax.sharding import PartitionSpec as P


def soft_terms(scores):
    largest = jnp.max(scores, axis=-1, keepdims=True)
    raised = jnp.exp(scores - largest)
    totals = jnp.sum(raised, axis=-1, keepdims=True)
    maxima = largest[..., 0] + jnp.log(totals[..., 0])
    weights = (raised / totals).astype(jnp.bfloat16)
    return (maxima, weights)


def contrast(maxima, positive):
    similarity = jnp.sum(maxima, axis=2)
    largest = jnp.max(similarity, axis=1, keepdims=True)
    raised = jnp.exp(similarity - largest)
    totals = jnp.sum(raised, axis=1, keepdims=True)
    picked = jnp.arange(similarity.shape[1], dtype=jnp.int32)[None, :] == positive[:, None]
    losses = (
        largest[:, 0] + jnp.log(totals[:, 0]) - jnp.sum(jnp.where(picked, similarity, 0.0), axis=1)
    )
    coefficients = (raised / totals - picked.astype(jnp.float32)).astype(jnp.bfloat16)
    return (losses, coefficients)


def body(queries, passages, passage_home, candidates, positive):
    shards = lax.axis_size("bank")
    query_rows, query_len, feature_dim = queries.shape
    listed = candidates.shape[1]
    holdings = passages.shape[0]
    tile_len = passages.shape[1]
    entries = query_rows * listed
    capacity = 3 * entries // shards
    storage = passage_home[candidates].reshape(entries)
    owner_bank = storage // holdings
    local_slot = storage % holdings
    member = (owner_bank[:, None] == jnp.arange(shards, dtype=jnp.int32)[None, :]).astype(jnp.int32)
    position = jnp.sum((jnp.cumsum(member, axis=0) - member) * member, axis=1)
    target = owner_bank * capacity + position
    slot_table = (
        jnp.zeros((shards * capacity,), jnp.int32)
        .at[target]
        .set(local_slot)
        .reshape(shards, capacity)
    )
    requests = lax.all_to_all(slot_table, "bank", split_axis=0, concat_axis=0, tiled=True)
    gathered = passages[requests.reshape(-1)].reshape(
        requests.shape[0], requests.shape[1], tile_len * feature_dim
    )
    fetched = lax.all_to_all(gathered, "bank", split_axis=0, concat_axis=0, tiled=True)
    passage_tiles = fetched.reshape(shards * capacity, tile_len, feature_dim)[target].reshape(
        query_rows, listed, tile_len, feature_dim
    )
    scores = jnp.einsum(
        "qid,qkjd->qkij", queries, passage_tiles, preferred_element_type=jnp.float32
    )
    maxima, weights = soft_terms(scores)
    token_basis = jnp.einsum(
        "qkij,qkjd->qkid", weights, passage_tiles, preferred_element_type=jnp.float32
    ).astype(jnp.bfloat16)
    token_basis = token_basis.reshape(query_rows, listed, query_len * feature_dim)
    losses, coefficients = contrast(maxima, positive)
    gradient = jnp.einsum(
        "qk,qkd->qd", coefficients, token_basis, preferred_element_type=jnp.float32
    )
    return (losses, gradient.reshape(query_rows, query_len, feature_dim))


def solution(mesh):
    return jax.shard_map(
        body,
        mesh=mesh,
        in_specs=(
            P(("query", "bank"), None, None),
            P("bank", None, None),
            P(),
            P(("query", "bank"), None),
            P(("query", "bank")),
        ),
        out_specs=(P(("query", "bank")), P(("query", "bank"), None, None)),
        check_vma=False,
    )
```

profile of v0, /device:TPU:122, one launch (start us, length us, event | category | flops | bytes accessed | tf_op | source)
XLA Modules:
  0.0 501.8 jit_solution(1293603079175023816)
XLA Ops:
  0.6 0.7 compare_select_fusion
  1.5 1.7 gather_fusion
  3.3 0.2 reduce_window_sum.11
  3.4 0.2 select_reduce_fusion
  3.6 1.0 scatter_custom_fusion
  4.7 15.3 %all_to_all.14 = s32[32,1,12]{2,1,0:T(1,128)S(1)} all-to-all(s32[32,1,12]{2,1,0:T(1,128)S(1)} %bitcast.53), channel_id=1, replica_groups=mesh['query'=8,'bank'=32] {'bank'}, dimensions={0} | all-to-all | bytes 3072 | tf_op jit(solution)/shard_map/all_to_all | solution.py:49
  20.0 0.5 broadcast.167
  20.5 0.7 reduce.5
  21.2 0.1 reshape.165
  21.3 14.4 %gather_fusion.1 = bf16[384,128,128]{2,1,0:T(8,128)(2,1)} fusion(bf16[256,128,128]{2,1,0:T(8,128)(2,1)} %param.6, s32[1024]{0:T(1024)S(1)} %pad_clamp_fusion.1), kind=kCustom, calls=%fused_computation.1 | custom fusion | bytes 25167360 | tf_op jit(solution)/shard_map/gather | solution.py:50
  35.8 18.6 %reshape.166 = bf16[32,12,16384]{2,1,0:T(8,128)(2,1)} reshape(bf16[384,128,128]{2,1,0:T(8,128)(2,1)} %gather_fusion.1) | data formatting | bytes 25165824 | tf_op jit(solution)/shard_map/reshape | solution.py:50
  54.4 9.4 %all-to-all-start.1 = ((bf16[32,12,16384]{2,1,0:T(8,128)(2,1)}), bf16[32,12,16384]{2,1,0:T(8,128)(2,1)}, u32[]{:S(2)}, u32[]{:S(2)}) async-start(bf16[32,12,16384]{2,1,0:T(8,128)(2,1)} %reshape.166), calls=%async_computation.1 | async-start | bytes 33554432 | tf_op jit(solution)/shard_map/all_to_all | solution.py:53
  63.8 401.8 %all-to-all-done.1 = bf16[32,12,16384]{2,1,0:T(8,128)(2,1)} async-done(((bf16[32,12,16384]{2,1,0:T(8,128)(2,1)}), bf16[32,12,16384]{2,1,0:T(8,128)(2,1)}, u32[]{:S(2)}, u32[]{:S(2)}) %all-to-all-start.1) | async-done | bytes 12582944 | tf_op jit(solution)/shard_map/all_to_all | solution.py:53
  465.7 19.1 %reshape.167 = bf16[384,128,128]{2,1,0:T(8,128)(2,1)} reshape(bf16[32,12,16384]{2,1,0:T(8,128)(2,1)} %all-to-all-done.1) | data formatting | bytes 25165824 | tf_op jit(solution)/shard_map/reshape | solution.py:54
  484.8 7.6 %gather_fusion.2 = bf16[128,128,128]{2,1,0:T(8,128)(2,1)} fusion(bf16[384,128,128]{2,1,0:T(8,128)(2,1)} %reshape.167, s32[1024]{0:T(1024)S(1)} %pad_clamp_fusion), kind=kCustom, calls=%fused_computation.2 | custom fusion | bytes 8389120 | tf_op jit(solution)/shard_map/gather | solution.py:54
  492.3 4.0 bitcast_reduce_fusion
  496.3 1.3 fusion.1
  497.8 1.5 convolution_convert_fusion
  499.3 0.1 reduce_max.19
  499.4 0.2 fusion.9
  499.7 0.5 reshape.169
  500.2 0.3 fusion.7
  500.6 0.7 copy.17
  501.2 0.5 add_subtract_fusion
  (18 shorter events, 0.6 us)
Async XLA Ops:
  0.6 491.7 %copy-start = (bf16[8,32,128]{2,1,0:T(8,128)(2,1)S(1)}, bf16[8,32,128]{2,1,0:T(8,128)(2,1)}, u32[]{:S(2)}) copy-start(bf16[8,32,128]{2,1,0:T(8,128)(2,1)} %param.5) | copy-start | bytes 196612
  54.4 411.3 %all-to-all-start.1 = ((bf16[32,12,16384]{2,1,0:T(8,128)(2,1)}), bf16[32,12,16384]{2,1,0:T(8,128)(2,1)}, u32[]{:S(2)}, u32[]{:S(2)}) async-start(bf16[32,12,16384]{2,1,0:T(8,128)(2,1)} %reshape.166), calls=%async_computation.1 | async-start | bytes 33554432 | tf_op jit(solution)/shard_map/all_to_all | solution.py:53
  492.3 5.4 %copy-start.1 = (bf16[128,128,128]{2,1,0:T(8,128)(2,1)S(1)}, bf16[128,128,128]{2,1,0:T(8,128)(2,1)}, u32[]{:S(2)}) copy-start(bf16[128,128,128]{2,1,0:T(8,128)(2,1)} %gather_fusion.2) | copy-start | bytes 12582916
  497.7 1.6 copy-start.2
where the time goes:
time: 503 us; the launch traced here: 502 us
  waiting for transfers between devices  402 us (80%)
  local copies, waits for them, and re-layouts  64.4 us (13%)
  blocking collectives  15.3 us (3%)
  starting transfers between devices  9.45 us (2%)
  matrix products  5.75 us (1%)
    all_to_all x1, waiting for transfers between devices, body(): lax.all_to_all(gathered, 'bank', split_axis=0, concat_axis=0, tiled=True)  402 us
    reshape x1, local copies, waits for them, and re-layouts, body(): fetched.reshape(shards * capacity, tile_len, feature_dim)[target]  19.1 us
    reshape x1, local copies, waits for them, and re-layouts, body(): passages[requests.reshape(-1)]  18.6 us
    all_to_all x1, blocking collectives, body(): lax.all_to_all(slot_table, 'bank', split_axis=0, concat_axis=0, tiled=True)  15.3 us
    gather x1, local copies, waits for them, and re-layouts, body(): passages[requests.reshape(-1)]  14.4 us
  transfers between devices with their start and end apart: 1, of which 1 were waited for; matrix products, arithmetic and copies ran while one was open for 0% of the time, Pallas kernels for 0%

commit v1 on v0

v1 whole, which is shorter than its diff:
```python
import jax
import jax.numpy as jnp
from jax import lax
from jax.sharding import PartitionSpec as P


def soft_terms(scores):
    largest = jnp.max(scores, axis=-1, keepdims=True)
    raised = jnp.exp(scores - largest)
    totals = jnp.sum(raised, axis=-1, keepdims=True)
    maxima = largest[..., 0] + jnp.log(totals[..., 0])
    weights = (raised / totals).astype(jnp.bfloat16)
    return (maxima, weights)


def contrast(similarity, positive):
    largest = jnp.max(similarity, axis=1, keepdims=True)
    raised = jnp.exp(similarity - largest)
    totals = jnp.sum(raised, axis=1, keepdims=True)
    picked = jnp.arange(similarity.shape[1], dtype=jnp.int32)[None, :] == positive[:, None]
    losses = (
        largest[:, 0] + jnp.log(totals[:, 0]) - jnp.sum(jnp.where(picked, similarity, 0.0), axis=1)
    )
    coefficients = (raised / totals - picked.astype(jnp.float32)).astype(jnp.bfloat16)
    return (losses, coefficients)


def body(queries, passages, passage_home, candidates, positive):
    shards = lax.axis_size("bank")
    me = lax.axis_index("bank")
    query_rows, query_len, feature_dim = queries.shape
    listed = candidates.shape[1]
    holdings = passages.shape[0]
    tile_len = passages.shape[1]
    entries = query_rows * listed
    capacity = 3 * entries // shards
    group_rows = shards * query_rows

    lists = jnp.concatenate([candidates, positive[:, None]], axis=1)
    lists = lax.all_gather(lists, "bank", axis=0, tiled=True)
    group_candidates = lists[:, :listed]
    group_positive = lists[:, listed]
    group_queries = lax.all_gather(queries, "bank", axis=0, tiled=True)

    storage = passage_home[group_candidates].reshape(shards, entries)
    mine = (storage // holdings) == me
    position = jnp.cumsum(mine.astype(jnp.int32), axis=1) - 1
    slot_ids = jnp.arange(capacity, dtype=jnp.int32)
    hit = mine[:, None, :] & (position[:, None, :] == slot_ids[None, :, None])
    valid = jnp.any(hit, axis=2)
    entry_ids = jnp.arange(entries, dtype=jnp.int32)
    entry = jnp.sum(jnp.where(hit, entry_ids[None, None, :], 0), axis=2)
    local_slot = jnp.sum(jnp.where(hit, (storage % holdings)[:, None, :], 0), axis=2)
    source = jnp.arange(shards, dtype=jnp.int32)[:, None]
    query_index = (source * query_rows + entry // listed).reshape(-1)
    flat_index = (source * entries + entry).reshape(-1)
    valid = valid.reshape(-1)
    local_slot = local_slot.reshape(-1)

    passage_tiles = passages[local_slot]
    query_tiles = group_queries[query_index]
    scores = jnp.einsum(
        "sid,sjd->sij", query_tiles, passage_tiles, preferred_element_type=jnp.float32
    )
    maxima, weights = soft_terms(scores)
    token_basis = jnp.einsum(
        "sij,sjd->sid", weights, passage_tiles, preferred_element_type=jnp.float32
    ).astype(jnp.bfloat16)

    slot_similarity = jnp.sum(maxima, axis=1)
    place = flat_index[:, None] == jnp.arange(group_rows * listed, dtype=jnp.int32)[None, :]
    place = place & valid[:, None]
    similarity = jnp.sum(jnp.where(place, slot_similarity[:, None], 0.0), axis=0)
    similarity = lax.psum(similarity, "bank").reshape(group_rows, listed)

    losses, coefficients = contrast(similarity, group_positive)
    slot_coefficient = jnp.where(
        valid, coefficients.reshape(-1)[flat_index], jnp.zeros((), jnp.bfloat16)
    )
    owner = query_index[:, None] == jnp.arange(group_rows, dtype=jnp.int32)[None, :]
    spread = jnp.where(owner, slot_coefficient[:, None], jnp.zeros((), jnp.bfloat16))
    partial = jnp.einsum(
        "sq,sd->qd",
        spread,
        token_basis.reshape(-1, query_len * feature_dim),
        preferred_element_type=jnp.float32,
    )
    gradient = lax.psum_scatter(partial, "bank", scatter_dimension=0, tiled=True)
    own_losses = lax.dynamic_slice_in_dim(losses, me * query_rows, query_rows)
    return (own_losses, gradient.reshape(query_rows, query_len, feature_dim))


def solution(mesh):
    return jax.shard_map(
        body,
        mesh=mesh,
        in_specs=(
            P(("query", "bank"), None, None),
            P("bank", None, None),
            P(),
            P(("query", "bank"), None),
            P(("query", "bank")),
        ),
        out_specs=(P(("query", "bank")), P(("query", "bank"), None, None)),
        check_vma=False,
    )
```

time: 503 us -> 503 us (level)
  the two profiles are of different devices: /device:TPU:122 before, /device:TPU:4 now
where the time goes in v1:
time: 503 us; the launch traced here: 502 us
  waiting for transfers between devices  220 us (44%)
  blocking collectives  187 us (37%)
  local copies, waits for them, and re-layouts  48.2 us (10%)
  matrix products  21.9 us (4%)
  between operations  14.3 us (3%)
  other arithmetic  10.4 us (2%)
    reduce_scatter x1, waiting for transfers between devices, body(): lax.psum_scatter(partial, 'bank', scatter_dimension=0, tiled=True)  220 us
    psum x1, blocking collectives, body(): similarity = lax.psum(similarity, 'bank').reshape(group_rows, listed)  140 us
    all_gather x1, blocking collectives, body(): lists = lax.all_gather(lists, 'bank', axis=0, tiled=True)  46.7 us
    gather x1, local copies, waits for them, and re-layouts, body(): storage = passage_home[group_candidates].reshape(shards, entries)  23 us
    gather x1, local copies, waits for them, and re-layouts, body(): passage_tiles = passages[local_slot]  14.4 us
    dot_general x1, matrix products, body(): jnp.einsum('sid,sjd->sij', query_tiles, passage_tiles, preferred_element_...  11.3 us
  transfers between devices with their start and end apart: 2, of which 1 were waited for; matrix products, arithmetic and copies ran while one was open for 8% of the time, Pallas kernels for 0%

profile of v1, /device:TPU:4, one launch (start us, length us, event | category | flops | bytes accessed | tf_op | source)
XLA Modules:
  0.0 502.4 jit_solution(9782047059398808998)
XLA Ops:
  7.2 0.7 all-gather.2.cloned.1.call-update
  8.0 0.7 copy.13
  8.7 0.8 pad_add_fusion
  9.5 46.7 %all_gather.6 = s32[256,17]{1,0:T(8,128)S(1)} all-gather(s32[8,17]{1,0:T(8,128)S(1)} %pad_add_fusion), channel_id=1, replica_groups=mesh['query'=8,'bank'=32] {'bank'}, dimensions={0}, use_global_device_ids=true | all-gather | bytes 17952 | tf_op jit(solution)/shard_map/all_gather | solution.py:40
  56.3 23.0 %gather_fusion = s32[4096]{0:T(1024)S(1)} fusion(s32[8192]{0:T(1024)S(1)} %copy-done, s32[4096]{0:T(1024)S(1)} %broadcast_clamp_fusion), kind=kCustom, calls=%fused_computation | custom fusion | bytes 49152 | tf_op jit(solution)/shard_map/gather | solution.py:45
  79.4 0.3 reduce_window_sum.11
  79.7 0.5 select_reduce_fusion.1
  81.3 0.3 fusion.13
  81.7 0.1 and.84
  81.8 0.2 slice_reduce_fusion
  82.2 14.4 %gather_fusion.2 = bf16[384,128,128]{2,1,0:T(8,128)(2,1)} fusion(bf16[256,128,128]{2,1,0:T(8,128)(2,1)} %param.6, s32[1024]{0:T(1024)S(1)} %pad_clamp_fusion.1), kind=kCustom, calls=%fused_computation.2 | custom fusion | bytes 25167360 | tf_op jit(solution)/shard_map/gather | solution.py:60
  96.8 2.8 gather_fusion.1
  99.6 11.3 %fusion.30 = (f32[384,32]{1,0:T(8,128)S(1)}, f32[384,32,128]{2,1,0:T(8,128)}) fusion(bf16[384,32,128]{2,1,0:T(8,128)(2,1)S(1)} %gather_fusion.1, bf16[384,128,128]{2,1,0:T(8,128)(2,1)} %gather_fusion.2), kind=kOutput, calls=%fused_computation.76 | convolution fusion | flops 404213760 | bytes 22069248 | tf_op jit(solution)/shard_map/sid,sjd->sij/dot_general | solution.py:62
  110.9 5.8 %fusion.1 = f32[384,32]{1,0:T(8,128)S(1)} fusion(f32[384,32,128]{2,1,0:T(8,128)} %get-tuple-element.21, f32[384,32]{1,0:T(8,128)S(1)} %get-tuple-element.20), kind=kLoop, calls=%fused_computation.9 | loop fusion | flops 3133440 | bytes 6389760 | tf_op jit(solution)/shard_map/reduce_sum | solution.py:10
  116.8 0.2 add_reduce_fusion
  116.9 7.1 %fusion.8 = bf16[384,32,128]{2,1,0:T(8,128)(2,1)S(1)} fusion(bf16[384,128,128]{2,1,0:T(8,128)(2,1)} %gather_fusion.2, f32[384,32,128]{2,1,0:T(8,128)S(1)} %copy-done.1, f32[384,32]{1,0:T(8,128)S(1)} %fusion.1, f32[384,32]{1,0:T(8,128)S(1)} %get-tuple-element.20), kind=kOutput, calls=%fused_computation.16 | convolution fusion | flops 408944640 | bytes 22118400 | tf_op jit(solution)/shard_map/sij,sjd->sid/dot_general | solution.py:66
  124.1 1.9 select_reduce_fusion
  126.0 140.5 %psum.7 = f32[4096]{0:T(1024)S(1)} all-reduce(f32[4096]{0:T(1024)S(1)} %select_reduce_fusion), channel_id=1, replica_groups=mesh['query'=8,'bank'=32] {'bank'}, use_global_device_ids=true, to_apply=%region_8.9 | all-reduce | flops 4096 | bytes 32768 | tf_op jit(solution)/shard_map/psum | solution.py:74
  266.7 0.3 exponential_reduce_fusion
  267.4 2.8 gather_fusion.3
  270.3 3.4 fusion.3
  273.7 0.6 dynamic_slice.3
  274.3 219.6 %reduce-scatter.2.cloned.1.call-done = f32[8,4096]{1,0:T(8,128)} async-done(((f32[256,4096]{1,0:T(8,128)}), f32[8,4096]{1,0:T(8,128)}) %reduce-scatter.2.cloned.1.call-update) | async-done | bytes 131088 | tf_op jit(solution)/shard_map/reduce_scatter | solution.py:88
  493.9 1.6 copy.18
  (44 shorter events, 2.3 us)
Async XLA Ops:
  7.2 49.1 %copy-start = (s32[8192]{0:T(1024)S(1)}, s32[8192]{0:T(1024)}, u32[]{:S(2)}) copy-start(s32[8192]{0:T(1024)} %param.7) | copy-start | bytes 98308
  7.2 89.6 %all-gather.2.cloned.1.call-start = ((), (), s32[]{:S(2)}) async-start(), calls=%async_computation.1 | async-start | bytes 2162688 | tf_op jit(solution)/shard_map/all_gather | solution.py:43
  7.9 486.0 %reduce-scatter.2.cloned.1.call-start = ((), (), s32[]{:S(2)}) async-start(), calls=%async_computation.2 | async-start | bytes 4325376 | tf_op jit(solution)/shard_map/reduce_scatter | solution.py:88
  110.9 6.0 %copy-start.1 = (f32[384,32,128]{2,1,0:T(8,128)S(1)}, f32[384,32,128]{2,1,0:T(8,128)}, u32[]{:S(2)}) copy-start(f32[384,32,128]{2,1,0:T(8,128)} %get-tuple-element.21) | copy-start | bytes 18874372
Sparse Core Ops, SparseCore 0:
  10.6 80.7 all-gather.1
  273.8 220.0 reduce-scatter.1

commit v2 on v1

v2 whole, which is shorter than its diff:
```python
import jax
import jax.numpy as jnp
import numpy as np
from jax import lax
from jax.sharding import Mesh
from jax.sharding import PartitionSpec as P

BANK = ("z", "y")


def soft_terms(scores):
    largest = jnp.max(scores, axis=-1, keepdims=True)
    raised = jnp.exp(scores - largest)
    totals = jnp.sum(raised, axis=-1, keepdims=True)
    maxima = largest[..., 0] + jnp.log(totals[..., 0])
    weights = (raised / totals).astype(jnp.bfloat16)
    return (maxima, weights)


def contrast(similarity, positive):
    largest = jnp.max(similarity, axis=1, keepdims=True)
    raised = jnp.exp(similarity - largest)
    totals = jnp.sum(raised, axis=1, keepdims=True)
    picked = jnp.arange(similarity.shape[1], dtype=jnp.int32)[None, :] == positive[:, None]
    losses = (
        largest[:, 0] + jnp.log(totals[:, 0]) - jnp.sum(jnp.where(picked, similarity, 0.0), axis=1)
    )
    coefficients = (raised / totals - picked.astype(jnp.float32)).astype(jnp.bfloat16)
    return (losses, coefficients)


def split3(value):
    high = lax.reduce_precision(value, exponent_bits=8, mantissa_bits=7)
    rest = value - high
    middle = lax.reduce_precision(rest, exponent_bits=8, mantissa_bits=7)
    low = rest - middle
    return jnp.stack([high, middle, low], axis=-1).astype(jnp.bfloat16)


def join3(pieces):
    pieces = pieces.astype(jnp.float32)
    return (pieces[..., 0] + pieces[..., 1]) + pieces[..., 2]


def gather_bank(value):
    value = lax.all_gather(value, "y", axis=0, tiled=True)
    return lax.all_gather(value, "z", axis=0, tiled=True)


def body(queries, passages, passage_home, candidates, positive):
    shards = lax.axis_size(BANK)
    me = lax.axis_index(BANK)
    query_rows, query_len, feature_dim = queries.shape
    listed = candidates.shape[1]
    holdings = passages.shape[0]
    entries = query_rows * listed
    capacity = 3 * entries // shards
    width = query_len * feature_dim
    tail = 128

    lists = jnp.concatenate([candidates, positive[:, None]], axis=1)
    group_candidates = gather_bank(lists)[:, :listed]
    group_queries = gather_bank(queries)

    storage = passage_home[group_candidates].reshape(shards, entries)
    mine = (storage // holdings) == me
    position = jnp.cumsum(mine.astype(jnp.int32), axis=1) - 1
    slot_ids = jnp.arange(capacity, dtype=jnp.int32)
    hit = mine[:, None, :] & (position[:, None, :] == slot_ids[None, :, None])
    entry_ids = jnp.arange(entries, dtype=jnp.int32)
    entry = jnp.sum(jnp.where(hit, entry_ids[None, None, :], 0), axis=2)
    local_slot = jnp.sum(jnp.where(hit, (storage % holdings)[:, None, :], 0), axis=2)
    source = jnp.arange(shards, dtype=jnp.int32)[:, None]
    query_index = (source * query_rows + entry // listed).reshape(-1)
    local_slot = local_slot.reshape(-1)

    passage_tiles = passages[local_slot]
    query_tiles = group_queries[query_index]
    scores = jnp.einsum(
        "sid,sjd->sij", query_tiles, passage_tiles, preferred_element_type=jnp.float32
    )
    maxima, weights = soft_terms(scores)
    token_basis = jnp.einsum(
        "sij,sjd->sid", weights, passage_tiles, preferred_element_type=jnp.float32
    ).astype(jnp.bfloat16)
    slot_similarity = split3(jnp.sum(maxima, axis=1)).reshape(shards, capacity * 3)
    payload = jnp.concatenate(
        [
            token_basis.reshape(shards, capacity * width),
            slot_similarity,
            jnp.zeros((shards, tail - capacity * 3), jnp.bfloat16),
        ],
        axis=1,
    )
    returned = lax.all_to_all(payload, BANK, 0, 0, tiled=True)

    own_storage = passage_home[candidates].reshape(entries)
    holder = own_storage // holdings
    member = holder[:, None] == jnp.arange(shards, dtype=jnp.int32)[None, :]
    member = member.astype(jnp.int32)
    own_position = jnp.sum((jnp.cumsum(member, axis=0) - member) * member, axis=1)
    pieces = returned[:, capacity * width : capacity * width + capacity * 3]
    pieces = pieces.reshape(shards * capacity, 3)
    flat_slot = holder * capacity + own_position
    similarity = join3(pieces[flat_slot]).reshape(query_rows, listed)
    losses, coefficients = contrast(similarity, positive)
    slot_of = flat_slot.reshape(query_rows, listed)
    spread = jnp.arange(shards * capacity, dtype=jnp.int32)[None, None, :] == slot_of[:, :, None]
    spread = jnp.sum(
        jnp.where(spread, coefficients[:, :, None].astype(jnp.float32), 0.0), axis=1
    ).astype(jnp.bfloat16)
    bases = returned[:, : capacity * width].reshape(shards * capacity, width)
    gradient = jnp.einsum("qs,sd->qd", spread, bases, preferred_element_type=jnp.float32)
    return (losses, gradient.reshape(query_rows, query_len, feature_dim))


def solution(mesh):
    rows = mesh.shape["query"]
    bank = mesh.shape["bank"]
    across = 4 if bank % 4 == 0 else 1
    devices = np.asarray(mesh.devices).reshape(rows, bank // across, across)
    split_mesh = Mesh(devices, ("query",) + BANK)
    every = ("query",) + BANK
    return jax.shard_map(
        body,
        mesh=split_mesh,
        in_specs=(
            P(every, None, None),
            P(BANK, None, None),
            P(),
            P(every, None),
            P(every),
        ),
        out_specs=(P(every), P(every, None, None)),
        check_vma=False,
    )
```

time: 503 us -> 257 us (0.51)
  waiting for transfers between devices: 220 us -> 61.9 us
  blocking collectives: 187 us -> 54.7 us
  local copies, waits for them, and re-layouts: 48.2 us -> 85.2 us
  starting transfers between devices: 0.08 us -> 6.67 us
    reduce_scatter x1 -> x0, waiting for transfers between devices: 220 us -> none  [body(): lax.psum_scatter(partial, 'bank', scatter_dimension=0, tiled=True)]
    psum x1 -> x0, blocking collectives: 140 us -> none  [body(): similarity = lax.psum(similarity, 'bank').reshape(group_rows, listed)]
    all_to_all x0 -> x1, waiting for transfers between devices: none -> 61.9 us  [body(): returned = lax.all_to_all(payload, BANK, 0, 0, tiled=True)]
    unnamed x5 -> x18, local copies, waits for them, and re-layouts: 1.6 us -> 27.9 us
    reshape x1 -> x4, local copies, waits for them, and re-layouts: 0.09 us -> 12.1 us  [the longest x2 9.12 us: body(): bases = returned[:, :capacity * width].reshape(shards * capacity, width)]
    all_gather x1 -> x3, blocking collectives: 46.7 us -> 54.7 us  [the longest x1 28.2 us: gather_bank(): return lax.all_gather(value, 'z', axis=0, tiled=True)]
    all_to_all x0 -> x1, starting transfers between devices: none -> 6.63 us  [body(): returned = lax.all_to_all(payload, BANK, 0, 0, tiled=True)]
  transfers between devices with their start and end apart: 2 -> 2, of which waited for: 1 -> 1; matrix products, arithmetic and copies ran while one was open for 8% -> 17% of each run, Pallas kernels for 0% -> 0%
where the time goes in v2:
time: 257 us
  local copies, waits for them, and re-layouts  85.2 us (33%)
  waiting for transfers between devices  61.9 us (24%)
  blocking collectives  54.7 us (21%)
  matrix products  19.4 us (8%)
  other arithmetic  14.4 us (6%)
  between operations  14.4 us (6%)
  starting transfers between devices  6.67 us (3%)
    all_to_all x1, waiting for transfers between devices, body(): returned = lax.all_to_all(payload, BANK, 0, 0, tiled=True)  61.9 us
    all_gather x1, blocking collectives, gather_bank(): return lax.all_gather(value, 'z', axis=0, tiled=True)  28.2 us
    unnamed x18, local copies, waits for them, and re-layouts  27.9 us
    all_gather x2, blocking collectives, gather_bank(): value = lax.all_gather(value, 'y', axis=0, tiled=True)  26.5 us
    gather x1, local copies, waits for them, and re-layouts, body(): storage = passage_home[group_candidates].reshape(shards, entries)  23 us
    gather x1, local copies, waits for them, and re-layouts, body(): passage_tiles = passages[local_slot]  14.4 us
    dot_general x1, matrix products, body(): jnp.einsum('sid,sjd->sij', query_tiles, passage_tiles, preferred_element_...  11.3 us
    reshape x2, local copies, waits for them, and re-layouts, body(): bases = returned[:, :capacity * width].reshape(shards * capacity, width)  9.12 us
  transfers between devices with their start and end apart: 2, of which 1 were waited for; matrix products, arithmetic and copies ran while one was open for 17% of the time, Pallas kernels for 0%

profile of v2, /device:TPU:4, one launch (start us, length us, event | category | flops | bytes accessed | tf_op | source)
XLA Modules:
  0.0 256.7 jit_solution(14263057151190145409)
XLA Ops:
  7.2 14.5 %all_gather.12 = bf16[32,32,128]{2,1,0:T(8,128)(2,1)} all-gather(bf16[8,32,128]{2,1,0:T(8,128)(2,1)} %param.5), channel_id=1, replica_groups=mesh['query'=8,'z'=8,'y'=4] {'y'}, dimensions={0}, use_global_device_ids=true | all-gather | bytes 327680 | tf_op jit(solution)/shard_map/all_gather | solution.py:46
  21.7 0.7 copy.33
  22.4 0.8 pad_add_fusion
  23.2 12.0 %all_gather.14 = s32[32,17]{1,0:T(8,128)S(1)} all-gather(s32[8,17]{1,0:T(8,128)S(1)} %pad_add_fusion), channel_id=1, replica_groups=mesh['query'=8,'z'=8,'y'=4] {'y'}, dimensions={0}, use_global_device_ids=true | all-gather | bytes 2720 | tf_op jit(solution)/shard_map/all_gather | solution.py:46
  35.3 28.2 %all-gather = s32[8,32,17]{1,2,0:T(8,128)S(1)} all-gather(s32[1,32,17]{1,2,0:T(8,128)S(1)} %copy.34), channel_id=1, replica_groups=mesh['query'=8,'z'=8,'y'=4] {'z'}, dimensions={0}, use_global_device_ids=true | all-gather | bytes 19584 | tf_op jit(solution)/shard_map/all_gather | solution.py:47
  63.9 23.0 %gather_fusion = s32[4096]{0:T(1024)S(1)} fusion(s32[8192]{0:T(1024)S(1)} %copy-done, s32[4096]{0:T(1024)S(1)} %broadcast_clamp_fusion), kind=kCustom, calls=%fused_computation | custom fusion | bytes 49152 | tf_op jit(solution)/shard_map/gather | solution.py:65
  88.4 14.4 %gather_fusion.2 = bf16[384,128,128]{2,1,0:T(8,128)(2,1)} fusion(bf16[256,128,128]{2,1,0:T(8,128)(2,1)} %param.6, s32[1024]{0:T(1024)S(1)} %pad_clamp_fusion.2), kind=kCustom, calls=%fused_computation.2 | custom fusion | bytes 25167360 | tf_op jit(solution)/shard_map/gather | solution.py:77
  102.8 2.8 %gather_fusion.1 = bf16[384,32,128]{2,1,0:T(8,128)(2,1)S(1)} fusion(bf16[256,32,128]{2,1,0:T(8,128)(2,1)} %all-gather.3.cloned.1.call-done, s32[1024]{0:T(1024)S(1)} %pad_clamp_fusion.3), kind=kCustom, calls=%fused_computation.1 | custom fusion | bytes 6292992 | tf_op jit(solution)/shard_map/gather | solution.py:78
  105.7 11.3 %fusion.27 = (f32[384,32]{1,0:T(8,128)S(1)}, f32[384,32,128]{2,1,0:T(8,128)}) fusion(bf16[384,32,128]{2,1,0:T(8,128)(2,1)S(1)} %gather_fusion.1, bf16[384,128,128]{2,1,0:T(8,128)(2,1)} %gather_fusion.2), kind=kOutput, calls=%fused_computation.94 | convolution fusion | flops 404213760 | bytes 22069248 | tf_op jit(solution)/shard_map/sid,sjd->sij/dot_general | solution.py:79
  117.0 5.8 %fusion = f32[384,32]{1,0:T(8,128)S(1)} fusion(f32[384,32,128]{2,1,0:T(8,128)} %get-tuple-element.24, f32[384,32]{1,0:T(8,128)S(1)} %get-tuple-element.23), kind=kLoop, calls=%fused_computation.7 | loop fusion | flops 3133440 | bytes 6389760 | tf_op jit(solution)/shard_map/reduce_sum | solution.py:14
  122.9 7.1 %fusion.4 = bf16[384,32,128]{2,1,0:T(8,128)(2,1)S(1)} fusion(bf16[384,128,128]{2,1,0:T(8,128)(2,1)} %gather_fusion.2, f32[384,32,128]{2,1,0:T(8,128)S(1)} %copy-done.1, f32[384,32]{1,0:T(8,128)S(1)} %fusion, f32[384,32]{1,0:T(8,128)S(1)} %get-tuple-element.23), kind=kOutput, calls=%fused_computation.12 | convolution fusion | flops 408944640 | bytes 22118400 | tf_op jit(solution)/shard_map/sij,sjd->sid/dot_general | solution.py:83
  130.2 2.8 %reshape.480 = bf16[32,49152]{1,0:T(8,128)(2,1)} reshape(bf16[384,32,128]{2,1,0:T(8,128)(2,1)S(1)} %fusion.4) | data formatting | bytes 6291456 | tf_op jit(solution)/shard_map/reshape | solution.py:89
  133.0 2.1 constant_dynamic-update-slice_fusion
  135.9 1.7 copy-done.2
  138.1 5.0 %reduce.6 = bf16[32,49280]{1,0:T(8,128)(2,1)S(1)} reduce(bf16[32,1,49280]{2,0,1:T(8,128)(2,1)} %bitcast.63, bf16[]{:T(256)} %broadcast.445), dimensions={1}, to_apply=%copy.40.reduce_sub_computation | reduce | bytes 6307842 | tf_op jit(solution)/shard_map/all_to_all | solution.py:95
  143.1 3.6 %reshape.538 = bf16[32,2,24640]{2,1,0:T(2,128)(2,1)} reshape(bf16[32,49280]{1,0:T(8,128)(2,1)S(1)} %reduce.6) | data formatting | bytes 6307840
  146.7 6.6 %all-to-all-start = ((bf16[32,2,24640]{2,1,0:T(2,128)(2,1)}), bf16[32,2,24640]{2,1,0:T(2,128)(2,1)S(1)}, u32[]{:S(2)}, u32[]{:S(2)}) async-start(bf16[32,2,24640]{2,1,0:T(2,128)(2,1)} %reshape.538), calls=%async_computation | async-start | bytes 6324224 | tf_op jit(solution)/shard_map/all_to_all | solution.py:95
  153.5 1.1 gather_fusion.3
  155.3 61.9 %all-to-all-done = bf16[32,2,24640]{2,1,0:T(2,128)(2,1)S(1)} async-done(((bf16[32,2,24640]{2,1,0:T(2,128)(2,1)}), bf16[32,2,24640]{2,1,0:T(2,128)(2,1)S(1)}, u32[]{:S(2)}, u32[]{:S(2)}) %all-to-all-start) | async-done | bytes 3153952 | tf_op jit(solution)/shard_map/all_to_all | solution.py:95
  217.2 16.4 %reshape.539 = bf16[32,1,49280]{2,1,0:T(2,128)(2,1)} reshape(bf16[32,2,24640]{2,1,0:T(2,128)(2,1)S(1)} %all-to-all-done) | data formatting | bytes 6307840
  233.5 3.1 %copy.45 = bf16[32,1,49280]{2,0,1:T(8,128)(2,1)S(1)} copy(bf16[32,1,49280]{2,1,0:T(2,128)(2,1)} %reshape.539) | data formatting | bytes 6307840
  239.0 5.7 %reshape.484 = bf16[384,4096]{1,0:T(8,128)(2,1)} reshape(bf16[32,49152]{1,0:T(8,128)(2,1)S(1)} %slice.39) | data formatting | bytes 6291456 | tf_op jit(solution)/shard_map/reshape | solution.py:112
  244.7 3.4 %copy.41 = bf16[384,4096]{0,1:T(8,128)(2,1)S(1)} copy(bf16[384,4096]{1,0:T(8,128)(2,1)} %reshape.484) | data formatting | bytes 6291456 | tf_op jit(solution)/shard_map/reshape | solution.py:112
  248.2 0.9 fusion.12
  (68 shorter events, 7.2 us)
Async XLA Ops:
  7.2 56.7 %copy-start = (s32[8192]{0:T(1024)S(1)}, s32[8192]{0:T(1024)}, u32[]{:S(2)}) copy-start(s32[8192]{0:T(1024)} %param.7) | copy-start | bytes 98308
  7.2 95.7 %all-gather.3.cloned.1.call-start = ((), (), s32[]{:S(2)}) async-start(), calls=%async_computation.1 | async-start | bytes 2359296 | tf_op jit(solution)/shard_map/all_gather | solution.py:47
  117.0 5.8 %copy-start.1 = (f32[384,32,128]{2,1,0:T(8,128)S(1)}, f32[384,32,128]{2,1,0:T(8,128)}, u32[]{:S(2)}) copy-start(f32[384,32,128]{2,1,0:T(8,128)} %get-tuple-element.24) | copy-start | bytes 18874372
  135.9 1.7 copy-start.2
  146.7 6.6 %copy-start.3 = (s32[8,16]{1,0:T(8,128)S(1)}, s32[8,16]{1,0:T(8,128)}, u32[]{:S(2)}) copy-start(s32[8,16]{1,0:T(8,128)} %param.8) | copy-start | bytes 1540
  146.7 70.5 %all-to-all-start = ((bf16[32,2,24640]{2,1,0:T(2,128)(2,1)}), bf16[32,2,24640]{2,1,0:T(2,128)(2,1)S(1)}, u32[]{:S(2)}, u32[]{:S(2)}) async-start(bf16[32,2,24640]{2,1,0:T(2,128)(2,1)} %reshape.538), calls=%async_computation | async-start | bytes 6324224 | tf_op jit(solution)/shard_map/all_to_all | solution.py:95
  236.7 1.5 copy-start.4
Sparse Core Ops, SparseCore 0:
  21.8 42.6 all-gather.2

commit v3 on v2

v3 whole, which is shorter than its diff:
```python
import functools

import jax
import jax.numpy as jnp
import numpy as np
from jax import lax
from jax.experimental import pallas as pl
from jax.experimental.pallas import tpu as pltpu
from jax.sharding import Mesh
from jax.sharding import PartitionSpec as P

BANK = ("z", "y")


def contrast(similarity, positive):
    largest = jnp.max(similarity, axis=1, keepdims=True)
    raised = jnp.exp(similarity - largest)
    totals = jnp.sum(raised, axis=1, keepdims=True)
    picked = jnp.arange(similarity.shape[1], dtype=jnp.int32)[None, :] == positive[:, None]
    losses = (
        largest[:, 0] + jnp.log(totals[:, 0]) - jnp.sum(jnp.where(picked, similarity, 0.0), axis=1)
    )
    coefficients = (raised / totals - picked.astype(jnp.float32)).astype(jnp.bfloat16)
    return (losses, coefficients)


def join3(pieces):
    pieces = pieces.astype(jnp.float32)
    return (pieces[..., 0] + pieces[..., 1]) + pieces[..., 2]


def gather_bank(value):
    value = lax.all_gather(value, "y", axis=0, tiled=True)
    return lax.all_gather(value, "z", axis=0, tiled=True)


def holder_kernel(capacity, slots_ref, picks_ref, queries_ref, *refs):
    tiles, out_ref = refs[:capacity], refs[capacity]
    source = pl.program_id(0)
    query_len, feature_dim = out_ref.shape[2], out_ref.shape[3]
    lane = lax.broadcasted_iota(jnp.int32, (1, feature_dim), 1)
    row = jnp.zeros((1, feature_dim), jnp.float32)
    for p in range(capacity):
        pick = picks_ref[source * capacity + p]
        query = queries_ref[pick]
        tile = tiles[p][0]
        scores = lax.dot_general(
            query, tile, (((1,), (1,)), ((), ())), preferred_element_type=jnp.float32
        )
        largest = jnp.max(scores, axis=1, keepdims=True)
        raised = jnp.exp(scores - largest)
        totals = jnp.sum(raised, axis=1, keepdims=True)
        maxima = largest + jnp.log(totals)
        weights = (raised / totals).astype(jnp.bfloat16)
        basis = jnp.dot(weights, tile, preferred_element_type=jnp.float32)
        out_ref[0, p] = basis.astype(jnp.bfloat16)
        similarity = jnp.sum(maxima, axis=0, keepdims=True)
        high = similarity.astype(jnp.bfloat16).astype(jnp.float32)
        rest = similarity - high
        middle = rest.astype(jnp.bfloat16).astype(jnp.float32)
        low = rest - middle
        row = jnp.where(lane == 3 * p, high, row)
        row = jnp.where(lane == 3 * p + 1, middle, row)
        row = jnp.where(lane == 3 * p + 2, low, row)
    sublane = lax.broadcasted_iota(jnp.int32, (query_len, feature_dim), 0)
    out_ref[0, capacity] = jnp.where(sublane == 0, row, 0.0).astype(jnp.bfloat16)


def holder_terms(slots, picks, group_queries, passages, shards, capacity):
    query_rows = group_queries.shape[0] // shards
    query_len, feature_dim = group_queries.shape[1], group_queries.shape[2]
    tile_len = passages.shape[1]

    def tile_spec(p):
        return pl.BlockSpec(
            (1, tile_len, feature_dim), lambda s, sl, pk: (sl[s * capacity + p], 0, 0)
        )

    grid_spec = pltpu.PrefetchScalarGridSpec(
        num_scalar_prefetch=2,
        grid=(shards,),
        in_specs=[pl.BlockSpec((query_rows, query_len, feature_dim), lambda s, sl, pk: (s, 0, 0))]
        + [tile_spec(p) for p in range(capacity)],
        out_specs=pl.BlockSpec(
            (1, capacity + 1, query_len, feature_dim), lambda s, sl, pk: (s, 0, 0, 0)
        ),
    )
    slots_total = shards * capacity
    flops = slots_total * 4 * query_len * tile_len * feature_dim
    moved = slots_total * (tile_len + query_len) * feature_dim * 2
    return pl.pallas_call(
        functools.partial(holder_kernel, capacity),
        grid_spec=grid_spec,
        out_shape=jax.ShapeDtypeStruct(
            (shards, capacity + 1, query_len, feature_dim), jnp.bfloat16
        ),
        cost_estimate=pl.CostEstimate(
            flops=flops, transcendentals=slots_total * query_len * tile_len, bytes_accessed=moved
        ),
    )(slots, picks, group_queries, *([passages] * capacity))


def body(queries, passages, passage_home, candidates, positive):
    shards = lax.axis_size(BANK)
    me = lax.axis_index(BANK)
    query_rows, query_len, feature_dim = queries.shape
    listed = candidates.shape[1]
    holdings = passages.shape[0]
    entries = query_rows * listed
    capacity = 3 * entries // shards
    width = query_len * feature_dim
    tail = 128

    own_storage = passage_home[candidates]
    holder = own_storage // holdings
    codes = jnp.concatenate(
        [holder, own_storage % holdings, jnp.zeros((query_rows, tail - 2 * listed), jnp.int32)],
        axis=1,
    ).astype(jnp.bfloat16)
    combined = jnp.concatenate([queries.reshape(query_rows, width), codes], axis=1)
    combined = gather_bank(combined)
    group_queries = combined[:, :width].reshape(shards * query_rows, query_len, feature_dim)
    group_codes = combined[:, width : width + 2 * listed].astype(jnp.int32)

    owner_bank = group_codes[:, :listed].reshape(shards, entries)
    stored_at = group_codes[:, listed:].reshape(shards, entries)
    mine = owner_bank == me
    position = jnp.cumsum(mine.astype(jnp.int32), axis=1) - 1
    slot_ids = jnp.arange(capacity, dtype=jnp.int32)
    hit = mine[:, None, :] & (position[:, None, :] == slot_ids[None, :, None])
    entry_ids = jnp.arange(entries, dtype=jnp.int32)
    entry = jnp.sum(jnp.where(hit, entry_ids[None, None, :], 0), axis=2)
    local_slot = jnp.sum(jnp.where(hit, stored_at[:, None, :], 0), axis=2)
    picks = (entry // listed).reshape(-1)
    payload = holder_terms(
        local_slot.reshape(-1), picks, group_queries, passages, shards, capacity
    )
    returned = lax.all_to_all(payload, BANK, 0, 0, tiled=True)

    holder = holder.reshape(entries)
    member = holder[:, None] == jnp.arange(shards, dtype=jnp.int32)[None, :]
    member = member.astype(jnp.int32)
    own_position = jnp.sum((jnp.cumsum(member, axis=0) - member) * member, axis=1)
    pieces = returned[:, capacity, 0, : capacity * 3].reshape(shards * capacity, 3)
    flat_slot = holder * capacity + own_position
    similarity = join3(pieces[flat_slot]).reshape(query_rows, listed)
    losses, coefficients = contrast(similarity, positive)
    slot_of = (holder * (capacity + 1) + own_position).reshape(query_rows, listed)
    rows = shards * (capacity + 1)
    spread = jnp.arange(rows, dtype=jnp.int32)[None, None, :] == slot_of[:, :, None]
    spread = jnp.sum(
        jnp.where(spread, coefficients[:, :, None].astype(jnp.float32), 0.0), axis=1
    ).astype(jnp.bfloat16)
    bases = returned.reshape(rows, query_len, feature_dim)
    gradient = jnp.einsum("qr,rid->qid", spread, bases, preferred_element_type=jnp.float32)
    return (losses, gradient)


def solution(mesh):
    rows = mesh.shape["query"]
    bank = mesh.shape["bank"]
    across = 4 if bank % 4 == 0 else 1
    devices = np.asarray(mesh.devices).reshape(rows, bank // across, across)
    split_mesh = Mesh(devices, ("query",) + BANK)
    every = ("query",) + BANK
    return jax.shard_map(
        body,
        mesh=split_mesh,
        in_specs=(
            P(every, None, None),
            P(BANK, None, None),
            P(),
            P(every, None),
            P(every),
        ),
        out_specs=(P(every), P(every, None, None)),
        check_vma=False,
    )
```

time: 257 us -> 302 us (1.18)
  Pallas kernels: 0 us -> 132 us
  local copies, waits for them, and re-layouts: 85.2 us -> 8.65 us
  waiting for transfers between devices: 61.9 us -> 118 us
  blocking collectives: 54.7 us -> 13.5 us
  matrix products: 19.4 us -> 1 us
  other arithmetic: 14.4 us -> 6.79 us
    pallas_call x0 -> x1, Pallas kernels: none -> 132 us  [holder_terms(): pl.pallas_call(functools.partial(holder_kernel, capacity), grid_spec=grid...]
    all_gather x1, waiting for transfers between devices: 0.02 us -> 43.4 us  [gather_bank(): return lax.all_gather(value, 'z', axis=0, tiled=True)]
    gather x5 -> x2, local copies, waits for them, and re-layouts: 41.5 us -> 1.23 us  [body(): own_storage = passage_home[candidates]]
    all_gather x1 -> x0, blocking collectives: 28.2 us -> none  [gather_bank(): return lax.all_gather(value, 'z', axis=0, tiled=True)]
    unnamed x18 -> x8, local copies, waits for them, and re-layouts: 27.9 us -> 4.32 us
    dot_general x3 -> x1, matrix products: 19.4 us -> 1 us  [body(): jnp.einsum('qr,rid->qid', spread, bases, preferred_element_type=jnp.float32)]
    all_gather x2 -> x1, blocking collectives: 26.5 us -> 13.5 us  [gather_bank(): value = lax.all_gather(value, 'y', axis=0, tiled=True)]
    all_to_all x1, waiting for transfers between devices: 61.9 us -> 74.6 us  [body(): returned = lax.all_to_all(payload, BANK, 0, 0, tiled=True)]
  transfers between devices with their start and end apart: 2 -> 2, of which waited for: 1 -> 2; matrix products, arithmetic and copies ran while one was open for 17% -> 0% of each run, Pallas kernels for 0% -> 0%
where the time goes in v3:
time: 302 us
  Pallas kernels  132 us (44%)
  waiting for transfers between devices  118 us (39%)
  between operations  14.2 us (5%)
  blocking collectives  13.5 us (4%)
  local copies, waits for them, and re-layouts  8.65 us (3%)
  starting transfers between devices  7.39 us (2%)
  other arithmetic  6.79 us (2%)
    pallas_call x1, Pallas kernels, holder_terms(): pl.pallas_call(functools.partial(holder_kernel, capacity), grid_spec=grid...  132 us
    all_to_all x1, waiting for transfers between devices, body(): returned = lax.all_to_all(payload, BANK, 0, 0, tiled=True)  74.6 us
    all_gather x1, waiting for transfers between devices, gather_bank(): return lax.all_gather(value, 'z', axis=0, tiled=True)  43.4 us
    all_gather x1, blocking collectives, gather_bank(): value = lax.all_gather(value, 'y', axis=0, tiled=True)  13.5 us
    all_to_all x1, starting transfers between devices, body(): returned = lax.all_to_all(payload, BANK, 0, 0, tiled=True)  7.35 us
  transfers between devices with their start and end apart: 2, of which 2 were waited for; matrix products, arithmetic and copies ran while one was open for 0% of the time, Pallas kernels for 0%

profile of v3, /device:TPU:4, one launch (start us, length us, event | category | flops | bytes accessed | tf_op | source)
XLA Modules:
  0.0 301.8 jit_solution(13111927301558813881)
XLA Ops:
  7.2 0.7 compare_select_fusion
  8.0 1.1 gather_fusion
  9.4 0.2 reduce_window_sum.23
  9.5 0.2 select_reduce_fusion.3
  10.0 13.5 %all_gather.6 = bf16[32,4224]{1,0:T(8,128)(2,1)} all-gather(bf16[8,4224]{1,0:T(8,128)(2,1)S(1)} %concatenate.6), channel_id=1, replica_groups=mesh['query'=8,'z'=8,'y'=4] {'y'}, dimensions={0}, use_global_device_ids=true | all-gather | bytes 337920 | tf_op jit(solution)/shard_map/all_gather | solution.py:33
  23.5 43.4 %all-gather.2.cloned.1.call-done = bf16[256,4224]{1,0:T(8,128)(2,1)} async-done(((bf16[32,4224]{1,0:T(8,128)(2,1)}), bf16[256,4224]{1,0:T(8,128)(2,1)}) %all-gather.2.cloned.1.call-update) | async-done | bytes 2162704 | tf_op jit(solution)/shard_map/all_gather | solution.py:34
  67.0 0.9 slice_convert_fusion
  68.1 0.3 reduce_window_sum.22
  68.5 0.5 select_reduce_fusion.1
  69.1 0.6 add_select_fusion.2.picks_ref
  69.8 0.7 reshape.252.slots_ref
  70.5 1.7 slice_bitcast_fusion
  72.3 1.9 copy.16
  74.1 132.2 %shard_map.68 = bf16[32,13,32,128]{3,2,1,0:T(8,128)(2,1)} custom-call(s32[384]{0:T(512)} %reshape.252.slots_ref, s32[384]{0:T(512)} %add_select_fusion.2.picks_ref, bf16[256,32,128]{2,1,0:T(8,128)(2,1)} %bitcast.28, bf16[256,128,128]{2,1,0:T(8,128)(2,1)} %refs_11_.1, bf16[256,128,128]{2,1,0:T(8,128)(2,1)} %refs_11_.1, bf16[256,128,128]{2,1,0:T(8,128)(2,1)} %refs_11_.1, ...), custom_call_target="tpu_custom_call" | custom-call | flops 805306368 | bytes 15728640 | tf_op jit(solution)/shard_map/pallas_call | solution.py:91
  206.3 7.3 %all-to-all-start = ((bf16[32,13,32,128]{3,2,1,0:T(8,128)(2,1)}), bf16[32,13,32,128]{3,2,1,0:T(8,128)(2,1)S(1)}, u32[]{:S(2)}, u32[]{:S(2)}) async-start(bf16[32,13,32,128]{3,2,1,0:T(8,128)(2,1)} %shard_map.68), calls=%async_computation | async-start | bytes 6815744 | tf_op jit(solution)/shard_map/all_to_all | solution.py:138
  213.7 74.6 %all-to-all-done = bf16[32,13,32,128]{3,2,1,0:T(8,128)(2,1)S(1)} async-done(((bf16[32,13,32,128]{3,2,1,0:T(8,128)(2,1)}), bf16[32,13,32,128]{3,2,1,0:T(8,128)(2,1)S(1)}, u32[]{:S(2)}, u32[]{:S(2)}) %all-to-all-start) | async-done | bytes 3407904 | tf_op jit(solution)/shard_map/all_to_all | solution.py:138
  288.5 1.3 gather_fusion.1
  289.8 0.8 convert_element_type.45
  290.6 0.2 fusion.3
  290.9 0.9 fusion.9
  291.8 0.7 fusion.12
  292.7 1.0 fusion
  293.7 0.7 copy.14
  294.4 0.5 add_subtract_fusion
  (32 shorter events, 1.7 us)
Async XLA Ops:
  7.2 0.9 copy-start
  7.2 2.6 copy-start.1
  7.2 59.8 %all-gather.2.cloned.1.call-start = ((), (), s32[]{:S(2)}) async-start(), calls=%async_computation.1 | async-start | bytes 2433024 | tf_op jit(solution)/shard_map/all_gather | solution.py:34
  206.3 81.9 %all-to-all-start = ((bf16[32,13,32,128]{3,2,1,0:T(8,128)(2,1)}), bf16[32,13,32,128]{3,2,1,0:T(8,128)(2,1)S(1)}, u32[]{:S(2)}, u32[]{:S(2)}) async-start(bf16[32,13,32,128]{3,2,1,0:T(8,128)(2,1)} %shard_map.68), calls=%async_computation | async-start | bytes 6815744 | tf_op jit(solution)/shard_map/all_to_all | solution.py:138
Sparse Core Ops, SparseCore 0:
  23.6 43.2 all-gather.1

commit v4 on v3

--- a/solution.py
+++ b/solution.py
@@ -34,26 +34,35 @@
     return lax.all_gather(value, "z", axis=0, tiled=True)
 
 
-def holder_kernel(capacity, slots_ref, picks_ref, queries_ref, *refs):
-    tiles, out_ref = refs[:capacity], refs[capacity]
+def holder_kernel(capacity, group, slots_ref, picks_ref, queries_ref, *refs):
+    tiles, (out_ref, scores_ref, weights_ref) = refs[:capacity], refs[capacity:]
     source = pl.program_id(0)
-    query_len, feature_dim = out_ref.shape[2], out_ref.shape[3]
+    query_rows, query_len, feature_dim = queries_ref.shape
+    tile_len = tiles[0].shape[1]
+
+    @pl.when(source == 0)
+    def _():
+        weights_ref[...] = jnp.zeros_like(weights_ref)
+
+    stacked = jnp.concatenate([tiles[p][0] for p in range(capacity)], axis=0)
+    block = queries_ref[...].reshape(query_rows * query_len, feature_dim)
+    scores_ref[...] = lax.dot_general(
+        block, stacked, (((1,), (1,)), ((), ())), preferred_element_type=jnp.float32
+    )
     lane = lax.broadcasted_iota(jnp.int32, (1, feature_dim), 1)
     row = jnp.zeros((1, feature_dim), jnp.float32)
     for p in range(capacity):
         pick = picks_ref[source * capacity + p]
-        query = queries_ref[pick]
-        tile = tiles[p][0]
-        scores = lax.dot_general(
-            query, tile, (((1,), (1,)), ((), ())), preferred_element_type=jnp.float32
-        )
+        first = pl.multiple_of(pick * query_len, query_len)
+        scores = scores_ref[pl.ds(first, query_len), pl.ds(p * tile_len, tile_len)]
         largest = jnp.max(scores, axis=1, keepdims=True)
         raised = jnp.exp(scores - largest)
         totals = jnp.sum(raised, axis=1, keepdims=True)
         maxima = largest + jnp.log(totals)
-        weights = (raised / totals).astype(jnp.bfloat16)
-        basis = jnp.dot(weights, tile, preferred_element_type=jnp.float32)
-        out_ref[0, p] = basis.astype(jnp.bfloat16)
+        g, r = p // group, p % group
+        weights_ref[g, r * query_len : (r + 1) * query_len, r * tile_len : (r + 1) * tile_len] = (
+            raised / totals
+        ).astype(jnp.bfloat16)
         similarity = jnp.sum(maxima, axis=0, keepdims=True)
         high = similarity.astype(jnp.bfloat16).astype(jnp.float32)
         rest = similarity - high
@@ -62,6 +71,15 @@
         row = jnp.where(lane == 3 * p, high, row)
         row = jnp.where(lane == 3 * p + 1, middle, row)
         row = jnp.where(lane == 3 * p + 2, low, row)
+    for g in range(capacity // group):
+        basis = jnp.dot(
+            weights_ref[g],
+            stacked[g * group * tile_len : (g + 1) * group * tile_len],
+            preferred_element_type=jnp.float32,
+        )
+        out_ref[0, g * group : (g + 1) * group] = basis.astype(jnp.bfloat16).reshape(
+            group, query_len, feature_dim
+        )
     sublane = lax.broadcasted_iota(jnp.int32, (query_len, feature_dim), 0)
     out_ref[0, capacity] = jnp.where(sublane == 0, row, 0.0).astype(jnp.bfloat16)
 
@@ -76,6 +94,7 @@
             (1, tile_len, feature_dim), lambda s, sl, pk: (sl[s * capacity + p], 0, 0)
         )
 
+    group = 4 if capacity % 4 == 0 else 1
     grid_spec = pltpu.PrefetchScalarGridSpec(
         num_scalar_prefetch=2,
         grid=(shards,),
@@ -84,12 +103,16 @@
         out_specs=pl.BlockSpec(
             (1, capacity + 1, query_len, feature_dim), lambda s, sl, pk: (s, 0, 0, 0)
         ),
+        scratch_shapes=[
+            pltpu.VMEM((query_rows * query_len, capacity * tile_len), jnp.float32),
+            pltpu.VMEM((capacity // group, group * query_len, group * tile_len), jnp.bfloat16),
+        ],
     )
     slots_total = shards * capacity
-    flops = slots_total * 4 * query_len * tile_len * feature_dim
+    flops = shards * 2 * feature_dim * capacity * tile_len * (query_rows * query_len + group * query_len)
     moved = slots_total * (tile_len + query_len) * feature_dim * 2
     return pl.pallas_call(
-        functools.partial(holder_kernel, capacity),
+        functools.partial(holder_kernel, capacity, group),
         grid_spec=grid_spec,
         out_shape=jax.ShapeDtypeStruct(
             (shards, capacity + 1, query_len, feature_dim), jnp.bfloat16

time: 302 us -> 207 us (0.69)
  Pallas kernels: 132 us -> 37.1 us
    pallas_call x1, Pallas kernels: 132 us -> 37.1 us  [holder_terms(): pl.pallas_call(functools.partial(holder_kernel, capacity, group), grid_sp...]
where the time goes in v4:
time: 207 us
  waiting for transfers between devices  118 us (57%)
  Pallas kernels  37.1 us (18%)
  between operations  14.2 us (7%)
  blocking collectives  13.5 us (7%)
  local copies, waits for them, and re-layouts  8.65 us (4%)
  starting transfers between devices  7.38 us (4%)
  other arithmetic  6.79 us (3%)
    all_to_all x1, waiting for transfers between devices, body(): returned = lax.all_to_all(payload, BANK, 0, 0, tiled=True)  74.5 us
    all_gather x1, waiting for transfers between devices, gather_bank(): return lax.all_gather(value, 'z', axis=0, tiled=True)  43.4 us
    pallas_call x1, Pallas kernels, holder_terms(): pl.pallas_call(functools.partial(holder_kernel, capacity, group), grid_sp...  37.1 us
    all_gather x1, blocking collectives, gather_bank(): value = lax.all_gather(value, 'y', axis=0, tiled=True)  13.5 us
    all_to_all x1, starting transfers between devices, body(): returned = lax.all_to_all(payload, BANK, 0, 0, tiled=True)  7.35 us
    unnamed x8, local copies, waits for them, and re-layouts  4.32 us
  transfers between devices with their start and end apart: 2, of which 2 were waited for; matrix products, arithmetic and copies ran while one was open for 0% of the time, Pallas kernels for 0%

profile of v4, /device:TPU:4, one launch (start us, length us, event | category | flops | bytes accessed | tf_op | source)
XLA Modules:
  0.0 206.6 jit_solution(5306642537457893142)
XLA Ops:
  7.2 0.7 compare_select_fusion
  8.0 1.1 gather_fusion
  9.4 0.2 reduce_window_sum.23
  9.5 0.2 select_reduce_fusion.3
  10.0 13.5 %all_gather.6 = bf16[32,4224]{1,0:T(8,128)(2,1)} all-gather(bf16[8,4224]{1,0:T(8,128)(2,1)S(1)} %concatenate.6), channel_id=1, replica_groups=mesh['query'=8,'z'=8,'y'=4] {'y'}, dimensions={0}, use_global_device_ids=true | all-gather | bytes 337920 | tf_op jit(solution)/shard_map/all_gather | solution.py:33
  23.5 43.4 %all-gather.2.cloned.1.call-done = bf16[256,4224]{1,0:T(8,128)(2,1)} async-done(((bf16[32,4224]{1,0:T(8,128)(2,1)}), bf16[256,4224]{1,0:T(8,128)(2,1)}) %all-gather.2.cloned.1.call-update) | async-done | bytes 2162704 | tf_op jit(solution)/shard_map/all_gather | solution.py:34
  67.0 0.9 slice_convert_fusion
  68.1 0.3 reduce_window_sum.22
  68.5 0.5 select_reduce_fusion.1
  69.1 0.6 add_select_fusion.2.picks_ref
  69.8 0.7 reshape.252.slots_ref
  70.5 1.7 slice_bitcast_fusion
  72.3 1.9 copy.16
  74.1 37.1 %shard_map.68 = bf16[32,13,32,128]{3,2,1,0:T(8,128)(2,1)} custom-call(s32[384]{0:T(512)} %reshape.252.slots_ref, s32[384]{0:T(512)} %add_select_fusion.2.picks_ref, bf16[256,32,128]{2,1,0:T(8,128)(2,1)} %bitcast.28, bf16[256,128,128]{2,1,0:T(8,128)(2,1)} %refs_11_.1, bf16[256,128,128]{2,1,0:T(8,128)(2,1)} %refs_11_.1, bf16[256,128,128]{2,1,0:T(8,128)(2,1)} %refs_11_.1, ...), custom_call_target="tpu_custom_call" | custom-call | flops 4831838208 | bytes 15728640 | tf_op jit(solution)/shard_map/pallas_call | solution.py:114
  111.2 7.3 %all-to-all-start = ((bf16[32,13,32,128]{3,2,1,0:T(8,128)(2,1)}), bf16[32,13,32,128]{3,2,1,0:T(8,128)(2,1)S(1)}, u32[]{:S(2)}, u32[]{:S(2)}) async-start(bf16[32,13,32,128]{3,2,1,0:T(8,128)(2,1)} %shard_map.68), calls=%async_computation | async-start | bytes 6815744 | tf_op jit(solution)/shard_map/all_to_all | solution.py:161
  118.6 74.5 %all-to-all-done = bf16[32,13,32,128]{3,2,1,0:T(8,128)(2,1)S(1)} async-done(((bf16[32,13,32,128]{3,2,1,0:T(8,128)(2,1)}), bf16[32,13,32,128]{3,2,1,0:T(8,128)(2,1)S(1)}, u32[]{:S(2)}, u32[]{:S(2)}) %all-to-all-start) | async-done | bytes 3407904 | tf_op jit(solution)/shard_map/all_to_all | solution.py:161
  193.3 1.3 gather_fusion.1
  194.6 0.8 convert_element_type.45
  195.4 0.2 fusion.3
  195.7 0.9 fusion.9
  196.6 0.7 fusion.12
  197.5 1.0 fusion
  198.5 0.7 copy.14
  199.2 0.5 add_subtract_fusion
  (32 shorter events, 1.7 us)
Async XLA Ops:
  7.2 0.9 copy-start
  7.2 2.6 %copy-start.1 = (bf16[8,32,128]{2,1,0:T(8,128)(2,1)S(1)}, bf16[8,32,128]{2,1,0:T(8,128)(2,1)}, u32[]{:S(2)}) copy-start(bf16[8,32,128]{2,1,0:T(8,128)(2,1)} %param.5) | copy-start | bytes 196612
  7.2 59.8 %all-gather.2.cloned.1.call-start = ((), (), s32[]{:S(2)}) async-start(), calls=%async_computation.1 | async-start | bytes 2433024 | tf_op jit(solution)/shard_map/all_gather | solution.py:34
  111.2 81.9 %all-to-all-start = ((bf16[32,13,32,128]{3,2,1,0:T(8,128)(2,1)}), bf16[32,13,32,128]{3,2,1,0:T(8,128)(2,1)S(1)}, u32[]{:S(2)}, u32[]{:S(2)}) async-start(bf16[32,13,32,128]{3,2,1,0:T(8,128)(2,1)} %shard_map.68), calls=%async_computation | async-start | bytes 6815744 | tf_op jit(solution)/shard_map/all_to_all | solution.py:161
Sparse Core Ops, SparseCore 0:
  23.6 43.2 all-gather.1

commit v5 on v4

--- a/solution.py
+++ b/solution.py
@@ -29,12 +29,24 @@
     return (pieces[..., 0] + pieces[..., 1]) + pieces[..., 2]
 
 
-def gather_bank(value):
-    value = lax.all_gather(value, "y", axis=0, tiled=True)
-    return lax.all_gather(value, "z", axis=0, tiled=True)
-
-
-def holder_kernel(capacity, group, slots_ref, picks_ref, queries_ref, *refs):
+def ring_gather(value, axis, size):
+    def shift(x, step):
+        return lax.ppermute(x, axis, [(i, (i + step) % size) for i in range(size)])
+
+    right, left = [value], [value]
+    for _ in range(size // 2):
+        right.append(shift(right[-1], 1))
+    for _ in range((size - 1) // 2):
+        left.append(shift(left[-1], -1))
+    return jnp.stack(right + left[1:][::-1], axis=0)
+
+
+def gather_bank(value, shape):
+    value = ring_gather(value, "y", shape[1])
+    return ring_gather(value, "z", shape[0])
+
+
+def holder_kernel(capacity, group, slots_ref, picks_ref, sources_ref, queries_ref, *refs):
     tiles, (out_ref, scores_ref, weights_ref) = refs[:capacity], refs[capacity:]
     source = pl.program_id(0)
     query_rows, query_len, feature_dim = queries_ref.shape
@@ -84,24 +96,24 @@
     out_ref[0, capacity] = jnp.where(sublane == 0, row, 0.0).astype(jnp.bfloat16)
 
 
-def holder_terms(slots, picks, group_queries, passages, shards, capacity):
+def holder_terms(slots, picks, sources, group_queries, passages, shards, capacity):
     query_rows = group_queries.shape[0] // shards
     query_len, feature_dim = group_queries.shape[1], group_queries.shape[2]
     tile_len = passages.shape[1]
 
     def tile_spec(p):
         return pl.BlockSpec(
-            (1, tile_len, feature_dim), lambda s, sl, pk: (sl[s * capacity + p], 0, 0)
+            (1, tile_len, feature_dim), lambda s, sl, pk, sr: (sl[s * capacity + p], 0, 0)
         )
 
     group = 4 if capacity % 4 == 0 else 1
     grid_spec = pltpu.PrefetchScalarGridSpec(
-        num_scalar_prefetch=2,
+        num_scalar_prefetch=3,
         grid=(shards,),
-        in_specs=[pl.BlockSpec((query_rows, query_len, feature_dim), lambda s, sl, pk: (s, 0, 0))]
+        in_specs=[pl.BlockSpec((query_rows, query_len, feature_dim), lambda s, sl, pk, sr: (s, 0, 0))]
         + [tile_spec(p) for p in range(capacity)],
         out_specs=pl.BlockSpec(
-            (1, capacity + 1, query_len, feature_dim), lambda s, sl, pk: (s, 0, 0, 0)
+            (1, capacity + 1, query_len, feature_dim), lambda s, sl, pk, sr: (sr[s], 0, 0, 0)
         ),
         scratch_shapes=[
             pltpu.VMEM((query_rows * query_len, capacity * tile_len), jnp.float32),
@@ -120,7 +132,7 @@
         cost_estimate=pl.CostEstimate(
             flops=flops, transcendentals=slots_total * query_len * tile_len, bytes_accessed=moved
         ),
-    )(slots, picks, group_queries, *([passages] * capacity))
+    )(slots, picks, sources, group_queries, *([passages] * capacity))
 
 
 def body(queries, passages, passage_home, candidates, positive):
@@ -141,7 +153,14 @@
         axis=1,
     ).astype(jnp.bfloat16)
     combined = jnp.concatenate([queries.reshape(query_rows, width), codes], axis=1)
-    combined = gather_bank(combined)
+    spans = (lax.axis_size("z"), lax.axis_size("y"))
+    combined = gather_bank(combined, spans).reshape(shards * query_rows, -1)
+    offset_z = jnp.arange(spans[0], dtype=jnp.int32)[:, None]
+    offset_y = jnp.arange(spans[1], dtype=jnp.int32)[None, :]
+    sources = (
+        (lax.axis_index("z") - offset_z) % spans[0] * spans[1]
+        + (lax.axis_index("y") - offset_y) % spans[1]
+    ).reshape(shards)
     group_queries = combined[:, :width].reshape(shards * query_rows, query_len, feature_dim)
     group_codes = combined[:, width : width + 2 * listed].astype(jnp.int32)
 
@@ -156,7 +175,7 @@
     local_slot = jnp.sum(jnp.where(hit, stored_at[:, None, :], 0), axis=2)
     picks = (entry // listed).reshape(-1)
     payload = holder_terms(
-        local_slot.reshape(-1), picks, group_queries, passages, shards, capacity
+        local_slot.reshape(-1), picks, sources, group_queries, passages, shards, capacity
     )
     returned = lax.all_to_all(payload, BANK, 0, 0, tiled=True)
 

time: 207 us -> 179 us (0.86)
  starting transfers between devices: 7.38 us -> 23.7 us
  waiting for transfers between devices: 118 us -> 102 us
  blocking collectives: 13.5 us -> 0 us
  between operations: 14.2 us -> 0.86 us
    all_gather x1 -> x0, waiting for transfers between devices: 43.4 us -> none  [gather_bank(): return lax.all_gather(value, 'z', axis=0, tiled=True)]
    ppermute x0 -> x10, waiting for transfers between devices: none -> 29.4 us  [shift(): return lax.ppermute(x, axis, [(i, (i + step) % size) for i in range(size)])]
    ppermute x0 -> x10, starting transfers between devices: none -> 16.5 us  [shift(): return lax.ppermute(x, axis, [(i, (i + step) % size) for i in range(size)])]
    all_gather x1 -> x0, blocking collectives: 13.5 us -> none  [gather_bank(): value = lax.all_gather(value, 'y', axis=0, tiled=True)]
    all_to_all x1, waiting for transfers between devices: 74.5 us -> 72.2 us  [body(): returned = lax.all_to_all(payload, BANK, 0, 0, tiled=True)]
    unnamed x8 -> x14, local copies, waits for them, and re-layouts: 4.32 us -> 3 us
  transfers between devices with their start and end apart: 2 -> 11, of which waited for: 2 -> 7; matrix products, arithmetic and copies ran while one was open for 0% -> 0% of each run, Pallas kernels for 0% -> 0%
where the time goes in v5:
time: 179 us
  waiting for transfers between devices  102 us (57%)
  Pallas kernels  37.3 us (21%)
  starting transfers between devices  23.7 us (13%)
  local copies, waits for them, and re-layouts  7.94 us (4%)
  other arithmetic  6.12 us (3%)
    all_to_all x1, waiting for transfers between devices, body(): returned = lax.all_to_all(payload, BANK, 0, 0, tiled=True)  72.2 us
    pallas_call x1, Pallas kernels, holder_terms(): pl.pallas_call(functools.partial(holder_kernel, capacity, group), grid_sp...  37.3 us
    ppermute x10, waiting for transfers between devices, shift(): return lax.ppermute(x, axis, [(i, (i + step) % size) for i in range(size)])  29.4 us
    ppermute x10, starting transfers between devices, shift(): return lax.ppermute(x, axis, [(i, (i + step) % size) for i in range(size)])  16.5 us
    all_to_all x1, starting transfers between devices, body(): returned = lax.all_to_all(payload, BANK, 0, 0, tiled=True)  7.19 us
  transfers between devices with their start and end apart: 11, of which 7 were waited for; matrix products, arithmetic and copies ran while one was open for 0% of the time, Pallas kernels for 0%

profile of v5, /device:TPU:4, one launch (start us, length us, event | category | flops | bytes accessed | tf_op | source)
XLA Modules:
  0.0 178.6 jit_solution(6866815914934560576)
XLA Ops:
  0.6 0.7 compare_select_fusion
  1.5 1.1 gather_fusion
  3.4 1.6 collective-permute-start
  5.0 1.7 collective-permute-start.2
  6.7 2.2 %collective-permute-done = bf16[8,4224]{1,0:T(8,128)(2,1)S(1)} collective-permute-done((bf16[8,4224]{1,0:T(8,128)(2,1)S(1)}, bf16[8,4224]{1,0:T(8,128)(2,1)S(1)}, u32[]{:S(2)}, u32[]{:S(2)}) %collective-permute-start) | collective-permute-done | bytes 67616 | tf_op jit(solution)/shard_map/ppermute | solution.py:34
  9.9 4.5 %collective-permute-done.1 = bf16[8,4224]{1,0:T(8,128)(2,1)S(1)} collective-permute-done((bf16[8,4224]{1,0:T(8,128)(2,1)S(1)}, bf16[8,4224]{1,0:T(8,128)(2,1)S(1)}, u32[]{:S(2)}, u32[]{:S(2)}) %collective-permute-start.1) | collective-permute-done | bytes 67616 | tf_op jit(solution)/shard_map/ppermute | solution.py:34
  14.5 2.0 %collective-permute-start.3 = (bf16[4,8,4224]{2,1,0:T(8,128)(2,1)S(1)}, bf16[4,8,4224]{2,1,0:T(8,128)(2,1)S(1)}, u32[]{:S(2)}, u32[]{:S(2)}) collective-permute-start(bf16[4,8,4224]{2,1,0:T(8,128)(2,1)S(1)} %pad_maximum_fusion), channel_id=1, source_target_pairs={{0,4},{4,8},{8,12},{12,16},{16,20},{20,24},{24,28},{28,0},{1,5},{5... | collective-permute-start | bytes 811016 | tf_op jit(solution)/shard_map/ppermute | solution.py:34
  16.5 4.0 %collective-permute-start.7 = (bf16[4,8,4224]{2,1,0:T(8,128)(2,1)S(1)}, bf16[4,8,4224]{2,1,0:T(8,128)(2,1)S(1)}, u32[]{:S(2)}, u32[]{:S(2)}) collective-permute-start(bf16[4,8,4224]{2,1,0:T(8,128)(2,1)S(1)} %pad_maximum_fusion), channel_id=1, source_target_pairs={{0,28},{4,0},{8,4},{12,8},{16,12},{20,16},{24,20},{28,24},{1,29},{... | collective-permute-start | bytes 811016 | tf_op jit(solution)/shard_map/ppermute | solution.py:34
  20.5 4.3 %collective-permute-done.3 = bf16[4,8,4224]{2,1,0:T(8,128)(2,1)S(1)} collective-permute-done((bf16[4,8,4224]{2,1,0:T(8,128)(2,1)S(1)}, bf16[4,8,4224]{2,1,0:T(8,128)(2,1)S(1)}, u32[]{:S(2)}, u32[]{:S(2)}) %collective-permute-start.3) | collective-permute-done | bytes 270368 | tf_op jit(solution)/shard_map/ppermute | solution.py:34
  24.9 3.3 %collective-permute-start.8 = (bf16[4,8,4224]{2,1,0:T(8,128)(2,1)S(1)}, bf16[4,8,4224]{2,1,0:T(8,128)(2,1)S(1)}, u32[]{:S(2)}, u32[]{:S(2)}) collective-permute-start(bf16[4,8,4224]{2,1,0:T(8,128)(2,1)S(1)} %collective-permute-done.7), channel_id=1, source_target_pairs={{0,28},{4,0},{8,4},{12,8},{16,12},{20,16},{24,20},{28,24},{1,29},{... | collective-permute-start | bytes 811016 | tf_op jit(solution)/shard_map/ppermute | solution.py:34
  28.2 4.9 %collective-permute-done.4 = bf16[4,8,4224]{2,1,0:T(8,128)(2,1)S(1)} collective-permute-done((bf16[4,8,4224]{2,1,0:T(8,128)(2,1)S(1)}, bf16[4,8,4224]{2,1,0:T(8,128)(2,1)S(1)}, u32[]{:S(2)}, u32[]{:S(2)}) %collective-permute-start.4) | collective-permute-done | bytes 270368 | tf_op jit(solution)/shard_map/ppermute | solution.py:34
  33.1 3.6 %collective-permute-start.9 = (bf16[4,8,4224]{2,1,0:T(8,128)(2,1)S(1)}, bf16[4,8,4224]{2,1,0:T(8,128)(2,1)S(1)}, u32[]{:S(2)}, u32[]{:S(2)}) collective-permute-start(bf16[4,8,4224]{2,1,0:T(8,128)(2,1)S(1)} %collective-permute-done.8), channel_id=1, source_target_pairs={{0,28},{4,0},{8,4},{12,8},{16,12},{20,16},{24,20},{28,24},{1,29},{... | collective-permute-start | bytes 811016 | tf_op jit(solution)/shard_map/ppermute | solution.py:34
  36.7 5.8 %collective-permute-done.5 = bf16[4,8,4224]{2,1,0:T(8,128)(2,1)S(1)} collective-permute-done((bf16[4,8,4224]{2,1,0:T(8,128)(2,1)S(1)}, bf16[4,8,4224]{2,1,0:T(8,128)(2,1)S(1)}, u32[]{:S(2)}, u32[]{:S(2)}) %collective-permute-start.5) | collective-permute-done | bytes 270368 | tf_op jit(solution)/shard_map/ppermute | solution.py:34
  42.6 7.6 %collective-permute-done.6 = bf16[4,8,4224]{2,1,0:T(8,128)(2,1)S(1)} collective-permute-done((bf16[4,8,4224]{2,1,0:T(8,128)(2,1)S(1)}, bf16[4,8,4224]{2,1,0:T(8,128)(2,1)S(1)}, u32[]{:S(2)}, u32[]{:S(2)}) %collective-permute-start.6) | collective-permute-done | bytes 270368 | tf_op jit(solution)/shard_map/ppermute | solution.py:34
  50.7 1.9 %copy.16 = bf16[32,8,32,128]{3,2,1,0:T(8,128)(2,1)} copy(bf16[32,8,32,128]{3,1,2,0:T(8,128)(2,1)S(1)} %slice_bitcast_fusion) | data formatting | bytes 4194304
  54.6 0.7 reshape.306.slots_ref
  55.2 37.3 %shard_map.68 = bf16[32,13,32,128]{3,2,1,0:T(8,128)(2,1)} custom-call(s32[384]{0:T(512)} %reshape.306.slots_ref, s32[384]{0:T(512)} %add_select_fusion.2.picks_ref, s32[32]{0:T(128)} %add.163.sources_ref, bf16[256,32,128]{2,1,0:T(8,128)(2,1)} %bitcast.49, bf16[256,128,128]{2,1,0:T(8,128)(2,1)} %refs_11_.1, bf16[256,128,128]{2,1,0:T(8,128)(2,1)} %refs_11_.1, ...), custom_call_target="tpu_custom_call" | custom-call | flops 4831838208 | bytes 15728640 | tf_op jit(solution)/shard_map/pallas_call | solution.py:126
  92.5 7.2 %all-to-all-start = ((bf16[32,13,32,128]{3,2,1,0:T(8,128)(2,1)}), bf16[32,13,32,128]{3,2,1,0:T(8,128)(2,1)S(1)}, u32[]{:S(2)}, u32[]{:S(2)}) async-start(bf16[32,13,32,128]{3,2,1,0:T(8,128)(2,1)} %shard_map.68), calls=%async_computation | async-start | bytes 6815744 | tf_op jit(solution)/shard_map/all_to_all | solution.py:180
  99.7 72.2 %all-to-all-done = bf16[32,13,32,128]{3,2,1,0:T(8,128)(2,1)S(1)} async-done(((bf16[32,13,32,128]{3,2,1,0:T(8,128)(2,1)}), bf16[32,13,32,128]{3,2,1,0:T(8,128)(2,1)S(1)}, u32[]{:S(2)}, u32[]{:S(2)}) %all-to-all-start) | async-done | bytes 3407904 | tf_op jit(solution)/shard_map/all_to_all | solution.py:180
  172.1 1.3 gather_fusion.1
  173.5 0.8 convert_element_type.45
  174.6 0.9 fusion.9
  175.5 0.7 fusion.12
  176.4 1.0 fusion
  (61 shorter events, 6.4 us)
Async XLA Ops:
  0.6 0.8 copy-start
  1.4 1.8 copy-start.1
  3.4 5.5 %collective-permute-start = (bf16[8,4224]{1,0:T(8,128)(2,1)S(1)}, bf16[8,4224]{1,0:T(8,128)(2,1)S(1)}, u32[]{:S(2)}, u32[]{:S(2)}) collective-permute-start(bf16[8,4224]{1,0:T(8,128)(2,1)S(1)} %concatenate.6), channel_id=1, source_target_pairs={{0,1},{1,2},{2,3},{3,0},{4,5},{5,6},{6,7},{7,4},{8,9},{9,10},{10,1... | collective-permute-start | bytes 202760 | tf_op jit(solution)/shard_map/ppermute | solution.py:34
  5.0 5.0 %collective-permute-start.2 = (bf16[8,4224]{1,0:T(8,128)(2,1)S(1)}, bf16[8,4224]{1,0:T(8,128)(2,1)S(1)}, u32[]{:S(2)}, u32[]{:S(2)}) collective-permute-start(bf16[8,4224]{1,0:T(8,128)(2,1)S(1)} %concatenate.6), channel_id=1, source_target_pairs={{0,3},{1,0},{2,1},{3,2},{4,7},{5,4},{6,5},{7,6},{8,11},{9,8},{10,9... | collective-permute-start | bytes 202760 | tf_op jit(solution)/shard_map/ppermute | solution.py:34
  8.9 5.5 %collective-permute-start.1 = (bf16[8,4224]{1,0:T(8,128)(2,1)S(1)}, bf16[8,4224]{1,0:T(8,128)(2,1)S(1)}, u32[]{:S(2)}, u32[]{:S(2)}) collective-permute-start(bf16[8,4224]{1,0:T(8,128)(2,1)S(1)} %collective-permute-done), channel_id=1, source_target_pairs={{0,1},{1,2},{2,3},{3,0},{4,5},{5,6},{6,7},{7,4},{8,9},{9,10},{10,1... | collective-permute-start | bytes 202760 | tf_op jit(solution)/shard_map/ppermute | solution.py:34
  14.5 10.4 %collective-permute-start.3 = (bf16[4,8,4224]{2,1,0:T(8,128)(2,1)S(1)}, bf16[4,8,4224]{2,1,0:T(8,128)(2,1)S(1)}, u32[]{:S(2)}, u32[]{:S(2)}) collective-permute-start(bf16[4,8,4224]{2,1,0:T(8,128)(2,1)S(1)} %pad_maximum_fusion), channel_id=1, source_target_pairs={{0,4},{4,8},{8,12},{12,16},{16,20},{20,24},{24,28},{28,0},{1,5},{5... | collective-permute-start | bytes 811016 | tf_op jit(solution)/shard_map/ppermute | solution.py:34
  16.5 8.4 %collective-permute-start.7 = (bf16[4,8,4224]{2,1,0:T(8,128)(2,1)S(1)}, bf16[4,8,4224]{2,1,0:T(8,128)(2,1)S(1)}, u32[]{:S(2)}, u32[]{:S(2)}) collective-permute-start(bf16[4,8,4224]{2,1,0:T(8,128)(2,1)S(1)} %pad_maximum_fusion), channel_id=1, source_target_pairs={{0,28},{4,0},{8,4},{12,8},{16,12},{20,16},{24,20},{28,24},{1,29},{... | collective-permute-start | bytes 811016 | tf_op jit(solution)/shard_map/ppermute | solution.py:34
  24.8 8.3 %collective-permute-start.4 = (bf16[4,8,4224]{2,1,0:T(8,128)(2,1)S(1)}, bf16[4,8,4224]{2,1,0:T(8,128)(2,1)S(1)}, u32[]{:S(2)}, u32[]{:S(2)}) collective-permute-start(bf16[4,8,4224]{2,1,0:T(8,128)(2,1)S(1)} %collective-permute-done.3), channel_id=1, source_target_pairs={{0,4},{4,8},{8,12},{12,16},{16,20},{20,24},{24,28},{28,0},{1,5},{5... | collective-permute-start | bytes 811016 | tf_op jit(solution)/shard_map/ppermute | solution.py:34
  24.9 8.3 %collective-permute-start.8 = (bf16[4,8,4224]{2,1,0:T(8,128)(2,1)S(1)}, bf16[4,8,4224]{2,1,0:T(8,128)(2,1)S(1)}, u32[]{:S(2)}, u32[]{:S(2)}) collective-permute-start(bf16[4,8,4224]{2,1,0:T(8,128)(2,1)S(1)} %collective-permute-done.7), channel_id=1, source_target_pairs={{0,28},{4,0},{8,4},{12,8},{16,12},{20,16},{24,20},{28,24},{1,29},{... | collective-permute-start | bytes 811016 | tf_op jit(solution)/shard_map/ppermute | solution.py:34
  33.1 9.5 %collective-permute-start.5 = (bf16[4,8,4224]{2,1,0:T(8,128)(2,1)S(1)}, bf16[4,8,4224]{2,1,0:T(8,128)(2,1)S(1)}, u32[]{:S(2)}, u32[]{:S(2)}) collective-permute-start(bf16[4,8,4224]{2,1,0:T(8,128)(2,1)S(1)} %collective-permute-done.4), channel_id=1, source_target_pairs={{0,4},{4,8},{8,12},{12,16},{16,20},{20,24},{24,28},{28,0},{1,5},{5... | collective-permute-start | bytes 811016 | tf_op jit(solution)/shard_map/ppermute | solution.py:34
  33.1 17.1 %collective-permute-start.9 = (bf16[4,8,4224]{2,1,0:T(8,128)(2,1)S(1)}, bf16[4,8,4224]{2,1,0:T(8,128)(2,1)S(1)}, u32[]{:S(2)}, u32[]{:S(2)}) collective-permute-start(bf16[4,8,4224]{2,1,0:T(8,128)(2,1)S(1)} %collective-permute-done.8), channel_id=1, source_target_pairs={{0,28},{4,0},{8,4},{12,8},{16,12},{20,16},{24,20},{28,24},{1,29},{... | collective-permute-start | bytes 811016 | tf_op jit(solution)/shard_map/ppermute | solution.py:34
  42.6 7.7 %collective-permute-start.6 = (bf16[4,8,4224]{2,1,0:T(8,128)(2,1)S(1)}, bf16[4,8,4224]{2,1,0:T(8,128)(2,1)S(1)}, u32[]{:S(2)}, u32[]{:S(2)}) collective-permute-start(bf16[4,8,4224]{2,1,0:T(8,128)(2,1)S(1)} %collective-permute-done.5), channel_id=1, source_target_pairs={{0,4},{4,8},{8,12},{12,16},{16,20},{20,24},{24,28},{28,0},{1,5},{5... | collective-permute-start | bytes 811016 | tf_op jit(solution)/shard_map/ppermute | solution.py:34
  92.5 79.5 %all-to-all-start = ((bf16[32,13,32,128]{3,2,1,0:T(8,128)(2,1)}), bf16[32,13,32,128]{3,2,1,0:T(8,128)(2,1)S(1)}, u32[]{:S(2)}, u32[]{:S(2)}) async-start(bf16[32,13,32,128]{3,2,1,0:T(8,128)(2,1)} %shard_map.68), calls=%async_computation | async-start | bytes 6815744 | tf_op jit(solution)/shard_map/all_to_all | solution.py:180

commit v6 on v5

--- a/solution.py
+++ b/solution.py
@@ -9,6 +9,7 @@
 from jax.sharding import Mesh
 from jax.sharding import PartitionSpec as P
 
+
 BANK = ("z", "y")
 
 
@@ -34,20 +35,15 @@
         return lax.ppermute(x, axis, [(i, (i + step) % size) for i in range(size)])
 
     right, left = [value], [value]
-    for _ in range(size // 2):
+    for hop in range(size // 2):
         right.append(shift(right[-1], 1))
-    for _ in range((size - 1) // 2):
-        left.append(shift(left[-1], -1))
-    return jnp.stack(right + left[1:][::-1], axis=0)
-
-
-def gather_bank(value, shape):
-    value = ring_gather(value, "y", shape[1])
-    return ring_gather(value, "z", shape[0])
+        if hop < (size - 1) // 2:
+            left.append(shift(left[-1], -1))
+    return right + left[1:][::-1]
 
 
 def holder_kernel(capacity, group, slots_ref, picks_ref, sources_ref, queries_ref, *refs):
-    tiles, (out_ref, scores_ref, weights_ref) = refs[:capacity], refs[capacity:]
+    tiles, (_, out_ref, scores_ref, weights_ref) = refs[:capacity], refs[capacity:]
     source = pl.program_id(0)
     query_rows, query_len, feature_dim = queries_ref.shape
     tile_len = tiles[0].shape[1]
@@ -96,7 +92,8 @@
     out_ref[0, capacity] = jnp.where(sublane == 0, row, 0.0).astype(jnp.bfloat16)
 
 
-def holder_terms(slots, picks, sources, group_queries, passages, shards, capacity):
+def holder_terms(slots, picks, sources, group_queries, passages, payload, capacity):
+    shards = sources.shape[0]
     query_rows = group_queries.shape[0] // shards
     query_len, feature_dim = group_queries.shape[1], group_queries.shape[2]
     tile_len = passages.shape[1]
@@ -111,7 +108,8 @@
         num_scalar_prefetch=3,
         grid=(shards,),
         in_specs=[pl.BlockSpec((query_rows, query_len, feature_dim), lambda s, sl, pk, sr: (s, 0, 0))]
-        + [tile_spec(p) for p in range(capacity)],
+        + [tile_spec(p) for p in range(capacity)]
+        + [pl.BlockSpec(memory_space=pl.ANY)],
         out_specs=pl.BlockSpec(
             (1, capacity + 1, query_len, feature_dim), lambda s, sl, pk, sr: (sr[s], 0, 0, 0)
         ),
@@ -126,16 +124,15 @@
     return pl.pallas_call(
         functools.partial(holder_kernel, capacity, group),
         grid_spec=grid_spec,
-        out_shape=jax.ShapeDtypeStruct(
-            (shards, capacity + 1, query_len, feature_dim), jnp.bfloat16
-        ),
+        out_shape=jax.ShapeDtypeStruct(payload.shape, payload.dtype),
+        input_output_aliases={4 + capacity: 0},
         cost_estimate=pl.CostEstimate(
             flops=flops, transcendentals=slots_total * query_len * tile_len, bytes_accessed=moved
         ),
-    )(slots, picks, sources, group_queries, *([passages] * capacity))
-
-
-def body(queries, passages, passage_home, candidates, positive):
+    )(slots, picks, sources, group_queries, *([passages] * capacity), payload)
+
+
+def terms(queries, passages, passage_home, candidates, positive):
     shards = lax.axis_size(BANK)
     me = lax.axis_index(BANK)
     query_rows, query_len, feature_dim = queries.shape
@@ -154,29 +151,38 @@
     ).astype(jnp.bfloat16)
     combined = jnp.concatenate([queries.reshape(query_rows, width), codes], axis=1)
     spans = (lax.axis_size("z"), lax.axis_size("y"))
-    combined = gather_bank(combined, spans).reshape(shards * query_rows, -1)
-    offset_z = jnp.arange(spans[0], dtype=jnp.int32)[:, None]
-    offset_y = jnp.arange(spans[1], dtype=jnp.int32)[None, :]
-    sources = (
-        (lax.axis_index("z") - offset_z) % spans[0] * spans[1]
-        + (lax.axis_index("y") - offset_y) % spans[1]
-    ).reshape(shards)
-    group_queries = combined[:, :width].reshape(shards * query_rows, query_len, feature_dim)
-    group_codes = combined[:, width : width + 2 * listed].astype(jnp.int32)
-
-    owner_bank = group_codes[:, :listed].reshape(shards, entries)
-    stored_at = group_codes[:, listed:].reshape(shards, entries)
-    mine = owner_bank == me
-    position = jnp.cumsum(mine.astype(jnp.int32), axis=1) - 1
-    slot_ids = jnp.arange(capacity, dtype=jnp.int32)
-    hit = mine[:, None, :] & (position[:, None, :] == slot_ids[None, :, None])
-    entry_ids = jnp.arange(entries, dtype=jnp.int32)
-    entry = jnp.sum(jnp.where(hit, entry_ids[None, None, :], 0), axis=2)
-    local_slot = jnp.sum(jnp.where(hit, stored_at[:, None, :], 0), axis=2)
-    picks = (entry // listed).reshape(-1)
-    payload = holder_terms(
-        local_slot.reshape(-1), picks, sources, group_queries, passages, shards, capacity
-    )
+    nearby = jnp.stack(ring_gather(combined, "y", spans[1]), axis=0)
+    arrivals = ring_gather(nearby, "z", spans[0])
+    offset_y = jnp.arange(spans[1], dtype=jnp.int32)
+    near_sources = (lax.axis_index("y") - offset_y) % spans[1]
+    payload = jnp.zeros((shards, capacity + 1, query_len, feature_dim), jnp.bfloat16)
+    half = spans[0] // 2
+    groups = [[0]] + [[d, spans[0] - d] for d in range(1, (spans[0] + 1) // 2)]
+    if spans[0] % 2 == 0:
+        groups.append([half])
+    for offsets in groups:
+        block = jnp.concatenate([arrivals[d] for d in offsets], axis=0)
+        block, payload = lax.optimization_barrier((block, payload))
+        count = len(offsets) * spans[1]
+        block = block.reshape(count * query_rows, width + tail)
+        group_queries = block[:, :width].reshape(count * query_rows, query_len, feature_dim)
+        group_codes = block[:, width : width + 2 * listed].astype(jnp.int32)
+        sources = jnp.concatenate(
+            [(lax.axis_index("z") - d) % spans[0] * spans[1] + near_sources for d in offsets]
+        )
+        owner_bank = group_codes[:, :listed].reshape(count, entries)
+        stored_at = group_codes[:, listed:].reshape(count, entries)
+        mine = owner_bank == me
+        position = jnp.cumsum(mine.astype(jnp.int32), axis=1) - 1
+        slot_ids = jnp.arange(capacity, dtype=jnp.int32)
+        hit = mine[:, None, :] & (position[:, None, :] == slot_ids[None, :, None])
+        entry_ids = jnp.arange(entries, dtype=jnp.int32)
+        entry = jnp.sum(jnp.where(hit, entry_ids[None, None, :], 0), axis=2)
+        local_slot = jnp.sum(jnp.where(hit, stored_at[:, None, :], 0), axis=2)
+        picks = (entry // listed).reshape(-1)
+        payload = holder_terms(
+            local_slot.reshape(-1), picks, sources, group_queries, passages, payload, capacity
+        )
     returned = lax.all_to_all(payload, BANK, 0, 0, tiled=True)
 
     holder = holder.reshape(entries)
@@ -206,7 +212,7 @@
     split_mesh = Mesh(devices, ("query",) + BANK)
     every = ("query",) + BANK
     return jax.shard_map(
-        body,
+        terms,
         mesh=split_mesh,
         in_specs=(
             P(every, None, None),

time: 179 us -> 183 us (1.022)
  waiting for transfers between devices: 102 us -> 79.9 us
  Pallas kernels: 37.3 us -> 46.5 us
  other arithmetic: 6.12 us -> 15 us
  local copies, waits for them, and re-layouts: 7.94 us -> 16.2 us
    ppermute x10, waiting for transfers between devices: 29.4 us -> 4.57 us  [shift(): return lax.ppermute(x, axis, [(i, (i + step) % size) for i in range(size)])]
    pallas_call x1 -> x5, Pallas kernels: 37.3 us -> 46.5 us  [holder_terms(): pl.pallas_call(functools.partial(holder_kernel, capacity, group), grid_sp...]
    all_to_all x1, waiting for transfers between devices: 72.2 us -> 75.3 us  [terms(): returned = lax.all_to_all(payload, BANK, 0, 0, tiled=True)]
    unnamed x14 -> x26, local copies, waits for them, and re-layouts: 3 us -> 5.53 us
    broadcast_in_dim x3 -> x8, local copies, waits for them, and re-layouts: 0.19 us -> 2.63 us  [the longest x1 2.16 us: terms(): jnp.zeros((shards, capacity + 1, query_len, feature_dim), jnp.bfloat16)]
    reshape x1 -> x5, local copies, waits for them, and re-layouts: 0.69 us -> 3 us  [terms(): local_slot.reshape(-1)]
    concatenate x0 -> x6, other arithmetic: none -> 2.05 us  [the longest x3 1.88 us: terms(): jnp.concatenate([(lax.axis_index('z') - d) % spans[0] * spans[1] + near_s...]
    select_n x5 -> x8, other arithmetic: 1.34 us -> 3.35 us  [the longest x5 2.6 us: terms(): picks = (entry // listed).reshape(-1)]
  transfers between devices with their start and end apart: 11 -> 11, of which waited for: 7 -> 2; matrix products, arithmetic and copies ran while one was open for 0% -> 5% of each run, Pallas kernels for 0% -> 22%
where the time goes in v6:
time: 183 us
  waiting for transfers between devices  79.9 us (44%)
  Pallas kernels  46.5 us (25%)
  starting transfers between devices  23 us (13%)
  local copies, waits for them, and re-layouts  16.2 us (9%)
  other arithmetic  15 us (8%)
    all_to_all x1, waiting for transfers between devices, terms(): returned = lax.all_to_all(payload, BANK, 0, 0, tiled=True)  75.3 us
    pallas_call x5, Pallas kernels, holder_terms(): pl.pallas_call(functools.partial(holder_kernel, capacity, group), grid_sp...  46.5 us
    ppermute x10, starting transfers between devices, shift(): return lax.ppermute(x, axis, [(i, (i + step) % size) for i in range(size)])  16.1 us
    all_to_all x1, starting transfers between devices, terms(): returned = lax.all_to_all(payload, BANK, 0, 0, tiled=True)  6.89 us
    unnamed x26, local copies, waits for them, and re-layouts  5.53 us
    ppermute x10, waiting for transfers between devices, shift(): return lax.ppermute(x, axis, [(i, (i + step) % size) for i in range(size)])  4.57 us
  transfers between devices with their start and end apart: 11, of which 2 were waited for; matrix products, arithmetic and copies ran while one was open for 5% of the time, Pallas kernels for 22%

profile of v6, /device:TPU:4, one launch (start us, length us, event | category | flops | bytes accessed | tf_op | source)
XLA Modules:
  0.0 182.6 jit_solution(7871356714506148198)
XLA Ops:
  1.5 1.1 gather_fusion
  4.4 1.6 collective-permute-start
  6.0 1.7 collective-permute-start.2
  11.0 4.5 %collective-permute-done.1 = bf16[8,4224]{1,0:T(8,128)(2,1)S(1)} collective-permute-done((bf16[8,4224]{1,0:T(8,128)(2,1)S(1)}, bf16[8,4224]{1,0:T(8,128)(2,1)S(1)}, u32[]{:S(2)}, u32[]{:S(2)}) %collective-permute-start.1) | collective-permute-done | bytes 67616 | tf_op jit(solution)/shard_map/ppermute | solution.py:35
  15.7 2.0 %collective-permute-start.3 = (bf16[4,8,4224]{2,1,0:T(8,128)(2,1)S(1)}, bf16[4,8,4224]{2,1,0:T(8,128)(2,1)S(1)}, u32[]{:S(2)}, u32[]{:S(2)}) collective-permute-start(bf16[4,8,4224]{2,1,0:T(8,128)(2,1)S(1)} %pad_maximum_fusion.3), channel_id=1, source_target_pairs={{0,4},{4,8},{8,12},{12,16},{16,20},{20,24},{24,28},{28,0},{1,5},{5... | collective-permute-start | bytes 811016 | tf_op jit(solution)/shard_map/ppermute | solution.py:35
  17.7 4.0 %collective-permute-start.7 = (bf16[4,8,4224]{2,1,0:T(8,128)(2,1)S(1)}, bf16[4,8,4224]{2,1,0:T(8,128)(2,1)S(1)}, u32[]{:S(2)}, u32[]{:S(2)}) collective-permute-start(bf16[4,8,4224]{2,1,0:T(8,128)(2,1)S(1)} %pad_maximum_fusion.3), channel_id=1, source_target_pairs={{0,28},{4,0},{8,4},{12,8},{16,12},{20,16},{24,20},{28,24},{1,29},{... | collective-permute-start | bytes 811016 | tf_op jit(solution)/shard_map/ppermute | solution.py:35
  24.9 2.2 %broadcast_in_dim.145.refs_12_ = bf16[32,13,32,128]{3,2,1,0:T(8,128)(2,1)} broadcast(bf16[]{:T(256)} %constant.171.clone.1), dimensions={} | broadcast | bytes 3407874 | tf_op jit(solution)/shard_map/broadcast_in_dim | solution.py:158
  27.0 6.7 %shard_map.68.refs_12_ = bf16[32,13,32,128]{3,2,1,0:T(8,128)(2,1)} custom-call(s32[48]{0:T(128)} %reshape.384.slots_ref, s32[48]{0:T(128)} %and_select_fusion.7.picks_ref, s32[4]{0:T(128)} %broadcast_add_fusion.12.sources_ref, bf16[32,32,128]{2,1,0:T(8,128)(2,1)} %bitcast.61, bf16[256,128,128]{2,1,0:T(8,128)(2,1)} %refs_11_.9, ...), custom_call_target="tpu_custom_call", output_to_operand_aliasing={{}: (16, {})} | custom-call | flops 603979776 | bytes 1966080 | tf_op jit(solution)/shard_map/pallas_call | solution.py:124
  34.0 0.9 copy.30
  36.7 3.2 %collective-permute-start.8 = (bf16[4,8,4224]{2,1,0:T(8,128)(2,1)S(1)}, bf16[4,8,4224]{2,1,0:T(8,128)(2,1)S(1)}, u32[]{:S(2)}, u32[]{:S(2)}) collective-permute-start(bf16[4,8,4224]{2,1,0:T(8,128)(2,1)S(1)} %collective-permute-done.7), channel_id=1, source_target_pairs={{0,28},{4,0},{8,4},{12,8},{16,12},{20,16},{24,20},{28,24},{1,29},{... | collective-permute-start | bytes 811016 | tf_op jit(solution)/shard_map/ppermute | solution.py:35
  40.4 11.0 %shard_map.69.refs_12_ = bf16[32,13,32,128]{3,2,1,0:T(8,128)(2,1)} custom-call(s32[96]{0:T(128)} %reshape.387.slots_ref, s32[96]{0:T(128)} %and_select_fusion.5.picks_ref, s32[8]{0:T(128)} %pad_add_fusion.sources_ref, bf16[64,32,128]{2,1,0:T(8,128)(2,1)} %bitcast.55, bf16[256,128,128]{2,1,0:T(8,128)(2,1)} %refs_11_.9, ...), custom_call_target="tpu_custom_call", output_to_operand_aliasing={{}: (16, {})} | custom-call | flops 1207959552 | bytes 3932160 | tf_op jit(solution)/shard_map/pallas_call | solution.py:124
  51.6 0.9 copy.31
  54.3 3.2 %collective-permute-start.9 = (bf16[4,8,4224]{2,1,0:T(8,128)(2,1)S(1)}, bf16[4,8,4224]{2,1,0:T(8,128)(2,1)S(1)}, u32[]{:S(2)}, u32[]{:S(2)}) collective-permute-start(bf16[4,8,4224]{2,1,0:T(8,128)(2,1)S(1)} %collective-permute-done.8), channel_id=1, source_target_pairs={{0,28},{4,0},{8,4},{12,8},{16,12},{20,16},{24,20},{28,24},{1,29},{... | collective-permute-start | bytes 811016 | tf_op jit(solution)/shard_map/ppermute | solution.py:35
  58.1 11.1 %shard_map.70.refs_12_ = bf16[32,13,32,128]{3,2,1,0:T(8,128)(2,1)} custom-call(s32[96]{0:T(128)} %reshape.390.slots_ref, s32[96]{0:T(128)} %and_select_fusion.4.picks_ref, s32[8]{0:T(128)} %pad_add_fusion.1.sources_ref, bf16[64,32,128]{2,1,0:T(8,128)(2,1)} %bitcast.56, bf16[256,128,128]{2,1,0:T(8,128)(2,1)} %refs_11_.9, ...), custom_call_target="tpu_custom_call", output_to_operand_aliasing={{}: (16, {})} | custom-call | flops 1207959552 | bytes 3932160 | tf_op jit(solution)/shard_map/pallas_call | solution.py:124
  69.4 0.9 copy.32
  72.6 11.1 %shard_map.71.refs_12_ = bf16[32,13,32,128]{3,2,1,0:T(8,128)(2,1)} custom-call(s32[96]{0:T(128)} %reshape.393.slots_ref, s32[96]{0:T(128)} %and_select_fusion.3.picks_ref, s32[8]{0:T(128)} %pad_add_fusion.2.sources_ref, bf16[64,32,128]{2,1,0:T(8,128)(2,1)} %bitcast.57, bf16[256,128,128]{2,1,0:T(8,128)(2,1)} %refs_11_.9, ...), custom_call_target="tpu_custom_call", output_to_operand_aliasing={{}: (16, {})} | custom-call | flops 1207959552 | bytes 3932160 | tf_op jit(solution)/shard_map/pallas_call | solution.py:124
  83.8 0.8 copy.33
  87.0 6.6 %shard_map.72 = bf16[32,13,32,128]{3,2,1,0:T(8,128)(2,1)} custom-call(s32[48]{0:T(128)} %reshape.396.slots_ref, s32[48]{0:T(128)} %and_select_fusion.2.picks_ref, s32[4]{0:T(128)} %get-tuple-element.43.sources_ref, bf16[32,32,128]{2,1,0:T(8,128)(2,1)} %bitcast.60, bf16[256,128,128]{2,1,0:T(8,128)(2,1)} %refs_11_.9, ...), custom_call_target="tpu_custom_call", output_to_operand_aliasing={{}: (16, {})} | custom-call | flops 603979776 | bytes 1966080 | tf_op jit(solution)/shard_map/pallas_call | solution.py:124
  93.6 6.9 %all-to-all-start = ((bf16[32,13,32,128]{3,2,1,0:T(8,128)(2,1)}), bf16[32,13,32,128]{3,2,1,0:T(8,128)(2,1)S(1)}, u32[]{:S(2)}, u32[]{:S(2)}) async-start(bf16[32,13,32,128]{3,2,1,0:T(8,128)(2,1)} %shard_map.72), calls=%async_computation | async-start | bytes 6815744 | tf_op jit(solution)/shard_map/all_to_all | solution.py:186
  100.6 75.3 %all-to-all-done = bf16[32,13,32,128]{3,2,1,0:T(8,128)(2,1)S(1)} async-done(((bf16[32,13,32,128]{3,2,1,0:T(8,128)(2,1)}), bf16[32,13,32,128]{3,2,1,0:T(8,128)(2,1)S(1)}, u32[]{:S(2)}, u32[]{:S(2)}) %all-to-all-start) | async-done | bytes 3407904 | tf_op jit(solution)/shard_map/all_to_all | solution.py:186
  176.1 1.3 gather_fusion.1
  177.4 0.8 convert_element_type.93
  178.6 0.9 fusion.13
  180.4 1.0 fusion
  (139 shorter events, 21.8 us)
Async XLA Ops:
  0.6 0.8 copy-start
  0.6 3.0 %copy-start.1 = (bf16[8,32,128]{2,1,0:T(8,128)(2,1)S(1)}, bf16[8,32,128]{2,1,0:T(8,128)(2,1)}, u32[]{:S(2)}) copy-start(bf16[8,32,128]{2,1,0:T(8,128)(2,1)} %param.5) | copy-start | bytes 196612
  2.6 0.5 copy-start.2
  3.6 0.7 copy-start.5
  4.4 5.6 %collective-permute-start = (bf16[8,4224]{1,0:T(8,128)(2,1)S(1)}, bf16[8,4224]{1,0:T(8,128)(2,1)S(1)}, u32[]{:S(2)}, u32[]{:S(2)}) collective-permute-start(bf16[8,4224]{1,0:T(8,128)(2,1)S(1)} %concatenate.24), channel_id=1, source_target_pairs={{0,1},{1,2},{2,3},{3,0},{4,5},{5,6},{6,7},{7,4},{8,9},{9,10},{10,1... | collective-permute-start | bytes 202760 | tf_op jit(solution)/shard_map/ppermute | solution.py:35
  6.0 5.0 %collective-permute-start.2 = (bf16[8,4224]{1,0:T(8,128)(2,1)S(1)}, bf16[8,4224]{1,0:T(8,128)(2,1)S(1)}, u32[]{:S(2)}, u32[]{:S(2)}) collective-permute-start(bf16[8,4224]{1,0:T(8,128)(2,1)S(1)} %concatenate.24), channel_id=1, source_target_pairs={{0,3},{1,0},{2,1},{3,2},{4,7},{5,4},{6,5},{7,6},{8,11},{9,8},{10,9... | collective-permute-start | bytes 202760 | tf_op jit(solution)/shard_map/ppermute | solution.py:35
  10.1 5.5 %collective-permute-start.1 = (bf16[8,4224]{1,0:T(8,128)(2,1)S(1)}, bf16[8,4224]{1,0:T(8,128)(2,1)S(1)}, u32[]{:S(2)}, u32[]{:S(2)}) collective-permute-start(bf16[8,4224]{1,0:T(8,128)(2,1)S(1)} %collective-permute-done), channel_id=1, source_target_pairs={{0,1},{1,2},{2,3},{3,0},{4,5},{5,6},{6,7},{7,4},{8,9},{9,10},{10,1... | collective-permute-start | bytes 202760 | tf_op jit(solution)/shard_map/ppermute | solution.py:35
  15.7 18.1 %collective-permute-start.3 = (bf16[4,8,4224]{2,1,0:T(8,128)(2,1)S(1)}, bf16[4,8,4224]{2,1,0:T(8,128)(2,1)S(1)}, u32[]{:S(2)}, u32[]{:S(2)}) collective-permute-start(bf16[4,8,4224]{2,1,0:T(8,128)(2,1)S(1)} %pad_maximum_fusion.3), channel_id=1, source_target_pairs={{0,4},{4,8},{8,12},{12,16},{16,20},{20,24},{24,28},{28,0},{1,5},{5... | collective-permute-start | bytes 811016 | tf_op jit(solution)/shard_map/ppermute | solution.py:35
  17.7 16.1 %collective-permute-start.7 = (bf16[4,8,4224]{2,1,0:T(8,128)(2,1)S(1)}, bf16[4,8,4224]{2,1,0:T(8,128)(2,1)S(1)}, u32[]{:S(2)}, u32[]{:S(2)}) collective-permute-start(bf16[4,8,4224]{2,1,0:T(8,128)(2,1)S(1)} %pad_maximum_fusion.3), channel_id=1, source_target_pairs={{0,28},{4,0},{8,4},{12,8},{16,12},{20,16},{24,20},{28,24},{1,29},{... | collective-permute-start | bytes 811016 | tf_op jit(solution)/shard_map/ppermute | solution.py:35
  36.7 14.7 %collective-permute-start.4 = (bf16[4,8,4224]{2,1,0:T(8,128)(2,1)S(1)}, bf16[4,8,4224]{2,1,0:T(8,128)(2,1)S(1)}, u32[]{:S(2)}, u32[]{:S(2)}) collective-permute-start(bf16[4,8,4224]{2,1,0:T(8,128)(2,1)S(1)} %collective-permute-done.3), channel_id=1, source_target_pairs={{0,4},{4,8},{8,12},{12,16},{16,20},{20,24},{24,28},{28,0},{1,5},{5... | collective-permute-start | bytes 811016 | tf_op jit(solution)/shard_map/ppermute | solution.py:35
  36.7 14.7 %collective-permute-start.8 = (bf16[4,8,4224]{2,1,0:T(8,128)(2,1)S(1)}, bf16[4,8,4224]{2,1,0:T(8,128)(2,1)S(1)}, u32[]{:S(2)}, u32[]{:S(2)}) collective-permute-start(bf16[4,8,4224]{2,1,0:T(8,128)(2,1)S(1)} %collective-permute-done.7), channel_id=1, source_target_pairs={{0,28},{4,0},{8,4},{12,8},{16,12},{20,16},{24,20},{28,24},{1,29},{... | collective-permute-start | bytes 811016 | tf_op jit(solution)/shard_map/ppermute | solution.py:35
  54.3 14.8 %collective-permute-start.5 = (bf16[4,8,4224]{2,1,0:T(8,128)(2,1)S(1)}, bf16[4,8,4224]{2,1,0:T(8,128)(2,1)S(1)}, u32[]{:S(2)}, u32[]{:S(2)}) collective-permute-start(bf16[4,8,4224]{2,1,0:T(8,128)(2,1)S(1)} %collective-permute-done.4), channel_id=1, source_target_pairs={{0,4},{4,8},{8,12},{12,16},{16,20},{20,24},{24,28},{28,0},{1,5},{5... | collective-permute-start | bytes 811016 | tf_op jit(solution)/shard_map/ppermute | solution.py:35
  54.3 14.8 %collective-permute-start.9 = (bf16[4,8,4224]{2,1,0:T(8,128)(2,1)S(1)}, bf16[4,8,4224]{2,1,0:T(8,128)(2,1)S(1)}, u32[]{:S(2)}, u32[]{:S(2)}) collective-permute-start(bf16[4,8,4224]{2,1,0:T(8,128)(2,1)S(1)} %collective-permute-done.8), channel_id=1, source_target_pairs={{0,28},{4,0},{8,4},{12,8},{16,12},{20,16},{24,20},{28,24},{1,29},{... | collective-permute-start | bytes 811016 | tf_op jit(solution)/shard_map/ppermute | solution.py:35
  72.1 11.6 %collective-permute-start.6 = (bf16[4,8,4224]{2,1,0:T(8,128)(2,1)S(1)}, bf16[4,8,4224]{2,1,0:T(8,128)(2,1)S(1)}, u32[]{:S(2)}, u32[]{:S(2)}) collective-permute-start(bf16[4,8,4224]{2,1,0:T(8,128)(2,1)S(1)} %collective-permute-done.5), channel_id=1, source_target_pairs={{0,4},{4,8},{8,12},{12,16},{16,20},{20,24},{24,28},{28,0},{1,5},{5... | collective-permute-start | bytes 811016 | tf_op jit(solution)/shard_map/ppermute | solution.py:35
  93.6 6.9 %copy-start.3 = (s32[128]{0:T(128)S(1)}, s32[128]{0:T(128)}, u32[]{:S(2)}) copy-start(s32[128]{0:T(128)} %copy-done.2) | copy-start | bytes 1540
  93.6 6.9 %copy-start.6 = (s32[128]{0:T(128)S(1)}, s32[128]{0:T(128)}, u32[]{:S(2)}) copy-start(s32[128]{0:T(128)} %copy-done.5) | copy-start | bytes 1540
  93.6 86.6 %copy-start.4 = (s32[8,16]{1,0:T(8,128)S(1)}, s32[8,16]{1,0:T(8,128)}, u32[]{:S(2)}) copy-start(s32[8,16]{1,0:T(8,128)} %get-tuple-element.40) | copy-start | bytes 1540
  93.6 82.3 %all-to-all-start = ((bf16[32,13,32,128]{3,2,1,0:T(8,128)(2,1)}), bf16[32,13,32,128]{3,2,1,0:T(8,128)(2,1)S(1)}, u32[]{:S(2)}, u32[]{:S(2)}) async-start(bf16[32,13,32,128]{3,2,1,0:T(8,128)(2,1)} %shard_map.72), calls=%async_computation | async-start | bytes 6815744 | tf_op jit(solution)/shard_map/all_to_all | solution.py:186

commit v7 on v5

--- a/solution.py
+++ b/solution.py
@@ -42,22 +42,35 @@
 
 
 def gather_bank(value, shape):
-    value = ring_gather(value, "y", shape[1])
-    return ring_gather(value, "z", shape[0])
-
-
-def holder_kernel(capacity, group, slots_ref, picks_ref, sources_ref, queries_ref, *refs):
-    tiles, (out_ref, scores_ref, weights_ref) = refs[:capacity], refs[capacity:]
-    source = pl.program_id(0)
-    query_rows, query_len, feature_dim = queries_ref.shape
-    tile_len = tiles[0].shape[1]
-
-    @pl.when(source == 0)
+    nearby = ring_gather(value, "y", shape[1])
+    order = (lax.axis_index("y") - jnp.arange(shape[1], dtype=jnp.int32)) % shape[1]
+    nearby = jnp.take(nearby, order, axis=0)
+    return ring_gather(nearby, "z", shape[0])
+
+
+def holder_kernel(capacity, group, per, slots_ref, picks_ref, sources_ref, queries_ref, *refs):
+    tiles, (out_ref, scores_ref, weights_ref) = refs[: per * capacity], refs[per * capacity :]
+
+    @pl.when(pl.program_id(0) == 0)
     def _():
         weights_ref[...] = jnp.zeros_like(weights_ref)
 
+    for unit in range(per):
+        source_terms(
+            capacity, group, per, unit, picks_ref, queries_ref,
+            tiles[unit * capacity : (unit + 1) * capacity], out_ref, scores_ref, weights_ref,
+        )
+
+
+def source_terms(capacity, group, per, unit, picks_ref, queries_ref, tiles, out_ref, scores_ref, weights_ref):
+    source = pl.program_id(0) * per + unit
+    query_rows = queries_ref.shape[0] // per
+    query_len, feature_dim = queries_ref.shape[1], queries_ref.shape[2]
+    tile_len = tiles[0].shape[1]
     stacked = jnp.concatenate([tiles[p][0] for p in range(capacity)], axis=0)
-    block = queries_ref[...].reshape(query_rows * query_len, feature_dim)
+    block = queries_ref[unit * query_rows : (unit + 1) * query_rows].reshape(
+        query_rows * query_len, feature_dim
+    )
     scores_ref[...] = lax.dot_general(
         block, stacked, (((1,), (1,)), ((), ())), preferred_element_type=jnp.float32
     )
@@ -89,31 +102,34 @@
             stacked[g * group * tile_len : (g + 1) * group * tile_len],
             preferred_element_type=jnp.float32,
         )
-        out_ref[0, g * group : (g + 1) * group] = basis.astype(jnp.bfloat16).reshape(
+        out_ref[unit, g * group : (g + 1) * group] = basis.astype(jnp.bfloat16).reshape(
             group, query_len, feature_dim
         )
     sublane = lax.broadcasted_iota(jnp.int32, (query_len, feature_dim), 0)
-    out_ref[0, capacity] = jnp.where(sublane == 0, row, 0.0).astype(jnp.bfloat16)
-
-
-def holder_terms(slots, picks, sources, group_queries, passages, shards, capacity):
+    out_ref[unit, capacity] = jnp.where(sublane == 0, row, 0.0).astype(jnp.bfloat16)
+
+
+def holder_terms(slots, picks, sources, group_queries, passages, shards, capacity, per):
     query_rows = group_queries.shape[0] // shards
+    steps = shards // per
     query_len, feature_dim = group_queries.shape[1], group_queries.shape[2]
     tile_len = passages.shape[1]
 
-    def tile_spec(p):
+    def tile_spec(t):
         return pl.BlockSpec(
-            (1, tile_len, feature_dim), lambda s, sl, pk, sr: (sl[s * capacity + p], 0, 0)
+            (1, tile_len, feature_dim), lambda s, sl, pk, sr: (sl[s * per * capacity + t], 0, 0)
         )
 
     group = 4 if capacity % 4 == 0 else 1
     grid_spec = pltpu.PrefetchScalarGridSpec(
         num_scalar_prefetch=3,
-        grid=(shards,),
-        in_specs=[pl.BlockSpec((query_rows, query_len, feature_dim), lambda s, sl, pk, sr: (s, 0, 0))]
-        + [tile_spec(p) for p in range(capacity)],
+        grid=(steps,),
+        in_specs=[
+            pl.BlockSpec((per * query_rows, query_len, feature_dim), lambda s, sl, pk, sr: (s, 0, 0))
+        ]
+        + [tile_spec(t) for t in range(per * capacity)],
         out_specs=pl.BlockSpec(
-            (1, capacity + 1, query_len, feature_dim), lambda s, sl, pk, sr: (sr[s], 0, 0, 0)
+            (per, capacity + 1, query_len, feature_dim), lambda s, sl, pk, sr: (sr[s], 0, 0, 0)
         ),
         scratch_shapes=[
             pltpu.VMEM((query_rows * query_len, capacity * tile_len), jnp.float32),
@@ -124,7 +140,7 @@
     flops = shards * 2 * feature_dim * capacity * tile_len * (query_rows * query_len + group * query_len)
     moved = slots_total * (tile_len + query_len) * feature_dim * 2
     return pl.pallas_call(
-        functools.partial(holder_kernel, capacity, group),
+        functools.partial(holder_kernel, capacity, group, per),
         grid_spec=grid_spec,
         out_shape=jax.ShapeDtypeStruct(
             (shards, capacity + 1, query_len, feature_dim), jnp.bfloat16
@@ -132,7 +148,7 @@
         cost_estimate=pl.CostEstimate(
             flops=flops, transcendentals=slots_total * query_len * tile_len, bytes_accessed=moved
         ),
-    )(slots, picks, sources, group_queries, *([passages] * capacity))
+    )(slots, picks, sources, group_queries, *([passages] * (per * capacity)))
 
 
 def body(queries, passages, passage_home, candidates, positive):
@@ -155,12 +171,8 @@
     combined = jnp.concatenate([queries.reshape(query_rows, width), codes], axis=1)
     spans = (lax.axis_size("z"), lax.axis_size("y"))
     combined = gather_bank(combined, spans).reshape(shards * query_rows, -1)
-    offset_z = jnp.arange(spans[0], dtype=jnp.int32)[:, None]
-    offset_y = jnp.arange(spans[1], dtype=jnp.int32)[None, :]
-    sources = (
-        (lax.axis_index("z") - offset_z) % spans[0] * spans[1]
-        + (lax.axis_index("y") - offset_y) % spans[1]
-    ).reshape(shards)
+    offset_z = jnp.arange(spans[0], dtype=jnp.int32)
+    sources = (lax.axis_index("z") - offset_z) % spans[0]
     group_queries = combined[:, :width].reshape(shards * query_rows, query_len, feature_dim)
     group_codes = combined[:, width : width + 2 * listed].astype(jnp.int32)
 
@@ -175,7 +187,7 @@
     local_slot = jnp.sum(jnp.where(hit, stored_at[:, None, :], 0), axis=2)
     picks = (entry // listed).reshape(-1)
     payload = holder_terms(
-        local_slot.reshape(-1), picks, sources, group_queries, passages, shards, capacity
+        local_slot.reshape(-1), picks, sources, group_queries, passages, shards, capacity, spans[1]
     )
     returned = lax.all_to_all(payload, BANK, 0, 0, tiled=True)
 

time: 179 us -> 177 us (0.989)
  Pallas kernels: 37.3 us -> 34.5 us
    pallas_call x1, Pallas kernels: 37.3 us -> 34.5 us  [holder_terms(): pl.pallas_call(functools.partial(holder_kernel, capacity, group, per), gr...]
where the time goes in v7:
time: 177 us
  waiting for transfers between devices  102 us (58%)
  Pallas kernels  34.5 us (19%)
  starting transfers between devices  23.7 us (13%)
  local copies, waits for them, and re-layouts  7.94 us (4%)
  other arithmetic  6.78 us (4%)
    all_to_all x1, waiting for transfers between devices, body(): returned = lax.all_to_all(payload, BANK, 0, 0, tiled=True)  72.4 us
    pallas_call x1, Pallas kernels, holder_terms(): pl.pallas_call(functools.partial(holder_kernel, capacity, group, per), gr...  34.5 us
    ppermute x10, waiting for transfers between devices, shift(): return lax.ppermute(x, axis, [(i, (i + step) % size) for i in range(size)])  29.3 us
    ppermute x10, starting transfers between devices, shift(): return lax.ppermute(x, axis, [(i, (i + step) % size) for i in range(size)])  16.7 us
    all_to_all x1, starting transfers between devices, body(): returned = lax.all_to_all(payload, BANK, 0, 0, tiled=True)  7.02 us
  transfers between devices with their start and end apart: 11, of which 7 were waited for; matrix products, arithmetic and copies ran while one was open for 0% of the time, Pallas kernels for 0%

profile of v7, /device:TPU:4, one launch (start us, length us, event | category | flops | bytes accessed | tf_op | source)
XLA Modules:
  0.0 176.5 jit_solution(2737737874845943199)
XLA Ops:
  0.6 0.7 compare_select_fusion
  1.5 1.1 gather_fusion
  3.4 1.6 collective-permute-start
  5.0 1.7 collective-permute-start.2
  6.7 2.2 %collective-permute-done = bf16[8,4224]{1,0:T(8,128)(2,1)S(1)} collective-permute-done((bf16[8,4224]{1,0:T(8,128)(2,1)S(1)}, bf16[8,4224]{1,0:T(8,128)(2,1)S(1)}, u32[]{:S(2)}, u32[]{:S(2)}) %collective-permute-start) | collective-permute-done | bytes 67616 | tf_op jit(solution)/shard_map/ppermute | solution.py:34
  9.8 4.6 %collective-permute-done.1 = bf16[8,4224]{1,0:T(8,128)(2,1)S(1)} collective-permute-done((bf16[8,4224]{1,0:T(8,128)(2,1)S(1)}, bf16[8,4224]{1,0:T(8,128)(2,1)S(1)}, u32[]{:S(2)}, u32[]{:S(2)}) %collective-permute-start.1) | collective-permute-done | bytes 67616 | tf_op jit(solution)/shard_map/ppermute | solution.py:34
  15.1 2.0 %collective-permute-start.3 = (bf16[4,8,4224]{2,1,0:T(8,128)(2,1)S(1)}, bf16[4,8,4224]{2,1,0:T(8,128)(2,1)S(1)}, u32[]{:S(2)}, u32[]{:S(2)}) collective-permute-start(bf16[4,8,4224]{2,1,0:T(8,128)(2,1)S(1)} %broadcast_select_fusion), channel_id=1, source_target_pairs={{0,4},{4,8},{8,12},{12,16},{16,20},{20,24},{24,28},{28,0},{1,5},{5... | collective-permute-start | bytes 811016 | tf_op jit(solution)/shard_map/ppermute | solution.py:34
  17.3 4.0 %collective-permute-start.7 = (bf16[4,8,4224]{2,1,0:T(8,128)(2,1)S(1)}, bf16[4,8,4224]{2,1,0:T(8,128)(2,1)S(1)}, u32[]{:S(2)}, u32[]{:S(2)}) collective-permute-start(bf16[4,8,4224]{2,1,0:T(8,128)(2,1)S(1)} %broadcast_select_fusion), channel_id=1, source_target_pairs={{0,28},{4,0},{8,4},{12,8},{16,12},{20,16},{24,20},{28,24},{1,29},{... | collective-permute-start | bytes 811016 | tf_op jit(solution)/shard_map/ppermute | solution.py:34
  21.3 4.2 %collective-permute-done.3 = bf16[4,8,4224]{2,1,0:T(8,128)(2,1)S(1)} collective-permute-done((bf16[4,8,4224]{2,1,0:T(8,128)(2,1)S(1)}, bf16[4,8,4224]{2,1,0:T(8,128)(2,1)S(1)}, u32[]{:S(2)}, u32[]{:S(2)}) %collective-permute-start.3) | collective-permute-done | bytes 270368 | tf_op jit(solution)/shard_map/ppermute | solution.py:34
  25.6 3.4 %collective-permute-start.8 = (bf16[4,8,4224]{2,1,0:T(8,128)(2,1)S(1)}, bf16[4,8,4224]{2,1,0:T(8,128)(2,1)S(1)}, u32[]{:S(2)}, u32[]{:S(2)}) collective-permute-start(bf16[4,8,4224]{2,1,0:T(8,128)(2,1)S(1)} %collective-permute-done.7), channel_id=1, source_target_pairs={{0,28},{4,0},{8,4},{12,8},{16,12},{20,16},{24,20},{28,24},{1,29},{... | collective-permute-start | bytes 811016 | tf_op jit(solution)/shard_map/ppermute | solution.py:34
  29.0 4.8 %collective-permute-done.4 = bf16[4,8,4224]{2,1,0:T(8,128)(2,1)S(1)} collective-permute-done((bf16[4,8,4224]{2,1,0:T(8,128)(2,1)S(1)}, bf16[4,8,4224]{2,1,0:T(8,128)(2,1)S(1)}, u32[]{:S(2)}, u32[]{:S(2)}) %collective-permute-start.4) | collective-permute-done | bytes 270368 | tf_op jit(solution)/shard_map/ppermute | solution.py:34
  33.8 3.7 %collective-permute-start.9 = (bf16[4,8,4224]{2,1,0:T(8,128)(2,1)S(1)}, bf16[4,8,4224]{2,1,0:T(8,128)(2,1)S(1)}, u32[]{:S(2)}, u32[]{:S(2)}) collective-permute-start(bf16[4,8,4224]{2,1,0:T(8,128)(2,1)S(1)} %collective-permute-done.8), channel_id=1, source_target_pairs={{0,28},{4,0},{8,4},{12,8},{16,12},{20,16},{24,20},{28,24},{1,29},{... | collective-permute-start | bytes 811016 | tf_op jit(solution)/shard_map/ppermute | solution.py:34
  37.5 5.7 %collective-permute-done.5 = bf16[4,8,4224]{2,1,0:T(8,128)(2,1)S(1)} collective-permute-done((bf16[4,8,4224]{2,1,0:T(8,128)(2,1)S(1)}, bf16[4,8,4224]{2,1,0:T(8,128)(2,1)S(1)}, u32[]{:S(2)}, u32[]{:S(2)}) %collective-permute-start.5) | collective-permute-done | bytes 270368 | tf_op jit(solution)/shard_map/ppermute | solution.py:34
  43.3 7.6 %collective-permute-done.6 = bf16[4,8,4224]{2,1,0:T(8,128)(2,1)S(1)} collective-permute-done((bf16[4,8,4224]{2,1,0:T(8,128)(2,1)S(1)}, bf16[4,8,4224]{2,1,0:T(8,128)(2,1)S(1)}, u32[]{:S(2)}, u32[]{:S(2)}) %collective-permute-start.6) | collective-permute-done | bytes 270368 | tf_op jit(solution)/shard_map/ppermute | solution.py:34
  51.4 1.9 %copy.16 = bf16[32,8,32,128]{3,2,1,0:T(8,128)(2,1)} copy(bf16[32,8,32,128]{3,1,2,0:T(8,128)(2,1)S(1)} %slice_bitcast_fusion) | data formatting | bytes 4194304
  55.2 0.7 reshape.317.slots_ref
  55.9 34.5 %shard_map.68 = bf16[32,13,32,128]{3,2,1,0:T(8,128)(2,1)} custom-call(s32[384]{0:T(512)} %reshape.317.slots_ref, s32[384]{0:T(512)} %add_select_fusion.2.picks_ref, s32[8]{0:T(128)} %and_select_fusion.2.sources_ref, bf16[256,32,128]{2,1,0:T(8,128)(2,1)} %bitcast.53, bf16[256,128,128]{2,1,0:T(8,128)(2,1)} %refs_47_.1, bf16[256,128,128]{2,1,0:T(8,128)(2,1)} %refs_47_.1, ...), custom_call_target="tpu_custom_call" | custom-call | flops 4831838208 | bytes 15728640 | tf_op jit(solution)/shard_map/pallas_call | solution.py:142
  90.4 7.0 %all-to-all-start = ((bf16[32,13,32,128]{3,2,1,0:T(8,128)(2,1)}), bf16[32,13,32,128]{3,2,1,0:T(8,128)(2,1)S(1)}, u32[]{:S(2)}, u32[]{:S(2)}) async-start(bf16[32,13,32,128]{3,2,1,0:T(8,128)(2,1)} %shard_map.68), calls=%async_computation | async-start | bytes 6815744 | tf_op jit(solution)/shard_map/all_to_all | solution.py:192
  97.5 72.4 %all-to-all-done = bf16[32,13,32,128]{3,2,1,0:T(8,128)(2,1)S(1)} async-done(((bf16[32,13,32,128]{3,2,1,0:T(8,128)(2,1)}), bf16[32,13,32,128]{3,2,1,0:T(8,128)(2,1)S(1)}, u32[]{:S(2)}, u32[]{:S(2)}) %all-to-all-start) | async-done | bytes 3407904 | tf_op jit(solution)/shard_map/all_to_all | solution.py:192
  170.1 1.3 gather_fusion.2
  171.4 0.8 convert_element_type.45
  172.5 0.9 fusion.10
  173.4 0.7 fusion.13
  174.3 1.0 fusion
  (63 shorter events, 7.0 us)
Async XLA Ops:
  0.6 0.8 copy-start
  1.4 1.8 %copy-start.1 = (bf16[8,32,128]{2,1,0:T(8,128)(2,1)S(1)}, bf16[8,32,128]{2,1,0:T(8,128)(2,1)}, u32[]{:S(2)}) copy-start(bf16[8,32,128]{2,1,0:T(8,128)(2,1)} %param.5) | copy-start | bytes 196612
  3.4 5.5 %collective-permute-start = (bf16[8,4224]{1,0:T(8,128)(2,1)S(1)}, bf16[8,4224]{1,0:T(8,128)(2,1)S(1)}, u32[]{:S(2)}, u32[]{:S(2)}) collective-permute-start(bf16[8,4224]{1,0:T(8,128)(2,1)S(1)} %concatenate.6), channel_id=1, source_target_pairs={{0,1},{1,2},{2,3},{3,0},{4,5},{5,6},{6,7},{7,4},{8,9},{9,10},{10,1... | collective-permute-start | bytes 202760 | tf_op jit(solution)/shard_map/ppermute | solution.py:34
  5.0 4.8 %collective-permute-start.2 = (bf16[8,4224]{1,0:T(8,128)(2,1)S(1)}, bf16[8,4224]{1,0:T(8,128)(2,1)S(1)}, u32[]{:S(2)}, u32[]{:S(2)}) collective-permute-start(bf16[8,4224]{1,0:T(8,128)(2,1)S(1)} %concatenate.6), channel_id=1, source_target_pairs={{0,3},{1,0},{2,1},{3,2},{4,7},{5,4},{6,5},{7,6},{8,11},{9,8},{10,9... | collective-permute-start | bytes 202760 | tf_op jit(solution)/shard_map/ppermute | solution.py:34
  8.9 5.5 %collective-permute-start.1 = (bf16[8,4224]{1,0:T(8,128)(2,1)S(1)}, bf16[8,4224]{1,0:T(8,128)(2,1)S(1)}, u32[]{:S(2)}, u32[]{:S(2)}) collective-permute-start(bf16[8,4224]{1,0:T(8,128)(2,1)S(1)} %collective-permute-done), channel_id=1, source_target_pairs={{0,1},{1,2},{2,3},{3,0},{4,5},{5,6},{6,7},{7,4},{8,9},{9,10},{10,1... | collective-permute-start | bytes 202760 | tf_op jit(solution)/shard_map/ppermute | solution.py:34
  15.1 10.4 %collective-permute-start.3 = (bf16[4,8,4224]{2,1,0:T(8,128)(2,1)S(1)}, bf16[4,8,4224]{2,1,0:T(8,128)(2,1)S(1)}, u32[]{:S(2)}, u32[]{:S(2)}) collective-permute-start(bf16[4,8,4224]{2,1,0:T(8,128)(2,1)S(1)} %broadcast_select_fusion), channel_id=1, source_target_pairs={{0,4},{4,8},{8,12},{12,16},{16,20},{20,24},{24,28},{28,0},{1,5},{5... | collective-permute-start | bytes 811016 | tf_op jit(solution)/shard_map/ppermute | solution.py:34
  17.3 8.3 %collective-permute-start.7 = (bf16[4,8,4224]{2,1,0:T(8,128)(2,1)S(1)}, bf16[4,8,4224]{2,1,0:T(8,128)(2,1)S(1)}, u32[]{:S(2)}, u32[]{:S(2)}) collective-permute-start(bf16[4,8,4224]{2,1,0:T(8,128)(2,1)S(1)} %broadcast_select_fusion), channel_id=1, source_target_pairs={{0,28},{4,0},{8,4},{12,8},{16,12},{20,16},{24,20},{28,24},{1,29},{... | collective-permute-start | bytes 811016 | tf_op jit(solution)/shard_map/ppermute | solution.py:34
  25.5 8.3 %collective-permute-start.4 = (bf16[4,8,4224]{2,1,0:T(8,128)(2,1)S(1)}, bf16[4,8,4224]{2,1,0:T(8,128)(2,1)S(1)}, u32[]{:S(2)}, u32[]{:S(2)}) collective-permute-start(bf16[4,8,4224]{2,1,0:T(8,128)(2,1)S(1)} %collective-permute-done.3), channel_id=1, source_target_pairs={{0,4},{4,8},{8,12},{12,16},{16,20},{20,24},{24,28},{28,0},{1,5},{5... | collective-permute-start | bytes 811016 | tf_op jit(solution)/shard_map/ppermute | solution.py:34
  25.6 8.3 %collective-permute-start.8 = (bf16[4,8,4224]{2,1,0:T(8,128)(2,1)S(1)}, bf16[4,8,4224]{2,1,0:T(8,128)(2,1)S(1)}, u32[]{:S(2)}, u32[]{:S(2)}) collective-permute-start(bf16[4,8,4224]{2,1,0:T(8,128)(2,1)S(1)} %collective-permute-done.7), channel_id=1, source_target_pairs={{0,28},{4,0},{8,4},{12,8},{16,12},{20,16},{24,20},{28,24},{1,29},{... | collective-permute-start | bytes 811016 | tf_op jit(solution)/shard_map/ppermute | solution.py:34
  33.8 9.5 %collective-permute-start.5 = (bf16[4,8,4224]{2,1,0:T(8,128)(2,1)S(1)}, bf16[4,8,4224]{2,1,0:T(8,128)(2,1)S(1)}, u32[]{:S(2)}, u32[]{:S(2)}) collective-permute-start(bf16[4,8,4224]{2,1,0:T(8,128)(2,1)S(1)} %collective-permute-done.4), channel_id=1, source_target_pairs={{0,4},{4,8},{8,12},{12,16},{16,20},{20,24},{24,28},{28,0},{1,5},{5... | collective-permute-start | bytes 811016 | tf_op jit(solution)/shard_map/ppermute | solution.py:34
  33.8 17.1 %collective-permute-start.9 = (bf16[4,8,4224]{2,1,0:T(8,128)(2,1)S(1)}, bf16[4,8,4224]{2,1,0:T(8,128)(2,1)S(1)}, u32[]{:S(2)}, u32[]{:S(2)}) collective-permute-start(bf16[4,8,4224]{2,1,0:T(8,128)(2,1)S(1)} %collective-permute-done.8), channel_id=1, source_target_pairs={{0,28},{4,0},{8,4},{12,8},{16,12},{20,16},{24,20},{28,24},{1,29},{... | collective-permute-start | bytes 811016 | tf_op jit(solution)/shard_map/ppermute | solution.py:34
  43.3 7.7 %collective-permute-start.6 = (bf16[4,8,4224]{2,1,0:T(8,128)(2,1)S(1)}, bf16[4,8,4224]{2,1,0:T(8,128)(2,1)S(1)}, u32[]{:S(2)}, u32[]{:S(2)}) collective-permute-start(bf16[4,8,4224]{2,1,0:T(8,128)(2,1)S(1)} %collective-permute-done.5), channel_id=1, source_target_pairs={{0,4},{4,8},{8,12},{12,16},{16,20},{20,24},{24,28},{28,0},{1,5},{5... | collective-permute-start | bytes 811016 | tf_op jit(solution)/shard_map/ppermute | solution.py:34
  90.4 79.4 %all-to-all-start = ((bf16[32,13,32,128]{3,2,1,0:T(8,128)(2,1)}), bf16[32,13,32,128]{3,2,1,0:T(8,128)(2,1)S(1)}, u32[]{:S(2)}, u32[]{:S(2)}) async-start(bf16[32,13,32,128]{3,2,1,0:T(8,128)(2,1)} %shard_map.68), calls=%async_computation | async-start | bytes 6815744 | tf_op jit(solution)/shard_map/all_to_all | solution.py:192

commit v8 on v7

--- a/solution.py
+++ b/solution.py
@@ -120,7 +120,7 @@
             (1, tile_len, feature_dim), lambda s, sl, pk, sr: (sl[s * per * capacity + t], 0, 0)
         )
 
-    group = 4 if capacity % 4 == 0 else 1
+    group = 2 if capacity % 2 == 0 else 1
     grid_spec = pltpu.PrefetchScalarGridSpec(
         num_scalar_prefetch=3,
         grid=(steps,),

time: 177 us -> 175 us (0.989)
  Pallas kernels: 34.5 us -> 32.5 us
    pallas_call x1, Pallas kernels: 34.5 us -> 32.5 us  [holder_terms(): pl.pallas_call(functools.partial(holder_kernel, capacity, group, per), gr...]
where the time goes in v8:
time: 175 us; the launch traced here: 174 us
  waiting for transfers between devices  102 us (58%)
  Pallas kernels  32.5 us (19%)
  starting transfers between devices  23.8 us (14%)
  local copies, waits for them, and re-layouts  7.94 us (5%)
  other arithmetic  6.78 us (4%)
    all_to_all x1, waiting for transfers between devices, body(): returned = lax.all_to_all(payload, BANK, 0, 0, tiled=True)  72.3 us
    pallas_call x1, Pallas kernels, holder_terms(): pl.pallas_call(functools.partial(holder_kernel, capacity, group, per), gr...  32.5 us
    ppermute x10, waiting for transfers between devices, shift(): return lax.ppermute(x, axis, [(i, (i + step) % size) for i in range(size)])  29.3 us
    ppermute x10, starting transfers between devices, shift(): return lax.ppermute(x, axis, [(i, (i + step) % size) for i in range(size)])  16.7 us
    all_to_all x1, starting transfers between devices, body(): returned = lax.all_to_all(payload, BANK, 0, 0, tiled=True)  7.04 us
  transfers between devices with their start and end apart: 11, of which 7 were waited for; matrix products, arithmetic and copies ran while one was open for 0% of the time, Pallas kernels for 0%

profile of v8, /device:TPU:4, one launch (start us, length us, event | category | flops | bytes accessed | tf_op | source)
XLA Modules:
  0.0 174.4 jit_solution(17080214159171876878)
XLA Ops:
  0.6 0.7 compare_select_fusion
  1.5 1.1 gather_fusion
  3.4 1.6 collective-permute-start
  5.0 1.7 collective-permute-start.2
  6.7 2.2 %collective-permute-done = bf16[8,4224]{1,0:T(8,128)(2,1)S(1)} collective-permute-done((bf16[8,4224]{1,0:T(8,128)(2,1)S(1)}, bf16[8,4224]{1,0:T(8,128)(2,1)S(1)}, u32[]{:S(2)}, u32[]{:S(2)}) %collective-permute-start) | collective-permute-done | bytes 67616 | tf_op jit(solution)/shard_map/ppermute | solution.py:34
  9.8 4.6 %collective-permute-done.1 = bf16[8,4224]{1,0:T(8,128)(2,1)S(1)} collective-permute-done((bf16[8,4224]{1,0:T(8,128)(2,1)S(1)}, bf16[8,4224]{1,0:T(8,128)(2,1)S(1)}, u32[]{:S(2)}, u32[]{:S(2)}) %collective-permute-start.1) | collective-permute-done | bytes 67616 | tf_op jit(solution)/shard_map/ppermute | solution.py:34
  15.1 2.0 %collective-permute-start.3 = (bf16[4,8,4224]{2,1,0:T(8,128)(2,1)S(1)}, bf16[4,8,4224]{2,1,0:T(8,128)(2,1)S(1)}, u32[]{:S(2)}, u32[]{:S(2)}) collective-permute-start(bf16[4,8,4224]{2,1,0:T(8,128)(2,1)S(1)} %broadcast_select_fusion), channel_id=1, source_target_pairs={{0,4},{4,8},{8,12},{12,16},{16,20},{20,24},{24,28},{28,0},{1,5},{5... | collective-permute-start | bytes 811016 | tf_op jit(solution)/shard_map/ppermute | solution.py:34
  17.3 4.0 %collective-permute-start.7 = (bf16[4,8,4224]{2,1,0:T(8,128)(2,1)S(1)}, bf16[4,8,4224]{2,1,0:T(8,128)(2,1)S(1)}, u32[]{:S(2)}, u32[]{:S(2)}) collective-permute-start(bf16[4,8,4224]{2,1,0:T(8,128)(2,1)S(1)} %broadcast_select_fusion), channel_id=1, source_target_pairs={{0,28},{4,0},{8,4},{12,8},{16,12},{20,16},{24,20},{28,24},{1,29},{... | collective-permute-start | bytes 811016 | tf_op jit(solution)/shard_map/ppermute | solution.py:34
  21.3 4.2 %collective-permute-done.3 = bf16[4,8,4224]{2,1,0:T(8,128)(2,1)S(1)} collective-permute-done((bf16[4,8,4224]{2,1,0:T(8,128)(2,1)S(1)}, bf16[4,8,4224]{2,1,0:T(8,128)(2,1)S(1)}, u32[]{:S(2)}, u32[]{:S(2)}) %collective-permute-start.3) | collective-permute-done | bytes 270368 | tf_op jit(solution)/shard_map/ppermute | solution.py:34
  25.6 3.4 %collective-permute-start.8 = (bf16[4,8,4224]{2,1,0:T(8,128)(2,1)S(1)}, bf16[4,8,4224]{2,1,0:T(8,128)(2,1)S(1)}, u32[]{:S(2)}, u32[]{:S(2)}) collective-permute-start(bf16[4,8,4224]{2,1,0:T(8,128)(2,1)S(1)} %collective-permute-done.7), channel_id=1, source_target_pairs={{0,28},{4,0},{8,4},{12,8},{16,12},{20,16},{24,20},{28,24},{1,29},{... | collective-permute-start | bytes 811016 | tf_op jit(solution)/shard_map/ppermute | solution.py:34
  29.0 4.8 %collective-permute-done.4 = bf16[4,8,4224]{2,1,0:T(8,128)(2,1)S(1)} collective-permute-done((bf16[4,8,4224]{2,1,0:T(8,128)(2,1)S(1)}, bf16[4,8,4224]{2,1,0:T(8,128)(2,1)S(1)}, u32[]{:S(2)}, u32[]{:S(2)}) %collective-permute-start.4) | collective-permute-done | bytes 270368 | tf_op jit(solution)/shard_map/ppermute | solution.py:34
  33.8 3.7 %collective-permute-start.9 = (bf16[4,8,4224]{2,1,0:T(8,128)(2,1)S(1)}, bf16[4,8,4224]{2,1,0:T(8,128)(2,1)S(1)}, u32[]{:S(2)}, u32[]{:S(2)}) collective-permute-start(bf16[4,8,4224]{2,1,0:T(8,128)(2,1)S(1)} %collective-permute-done.8), channel_id=1, source_target_pairs={{0,28},{4,0},{8,4},{12,8},{16,12},{20,16},{24,20},{28,24},{1,29},{... | collective-permute-start | bytes 811016 | tf_op jit(solution)/shard_map/ppermute | solution.py:34
  37.5 5.7 %collective-permute-done.5 = bf16[4,8,4224]{2,1,0:T(8,128)(2,1)S(1)} collective-permute-done((bf16[4,8,4224]{2,1,0:T(8,128)(2,1)S(1)}, bf16[4,8,4224]{2,1,0:T(8,128)(2,1)S(1)}, u32[]{:S(2)}, u32[]{:S(2)}) %collective-permute-start.5) | collective-permute-done | bytes 270368 | tf_op jit(solution)/shard_map/ppermute | solution.py:34
  43.3 7.6 %collective-permute-done.6 = bf16[4,8,4224]{2,1,0:T(8,128)(2,1)S(1)} collective-permute-done((bf16[4,8,4224]{2,1,0:T(8,128)(2,1)S(1)}, bf16[4,8,4224]{2,1,0:T(8,128)(2,1)S(1)}, u32[]{:S(2)}, u32[]{:S(2)}) %collective-permute-start.6) | collective-permute-done | bytes 270368 | tf_op jit(solution)/shard_map/ppermute | solution.py:34
  51.4 1.9 %copy.16 = bf16[32,8,32,128]{3,2,1,0:T(8,128)(2,1)} copy(bf16[32,8,32,128]{3,1,2,0:T(8,128)(2,1)S(1)} %slice_bitcast_fusion) | data formatting | bytes 4194304
  55.2 0.7 reshape.317.slots_ref
  55.9 32.5 %shard_map.68 = bf16[32,13,32,128]{3,2,1,0:T(8,128)(2,1)} custom-call(s32[384]{0:T(512)} %reshape.317.slots_ref, s32[384]{0:T(512)} %add_select_fusion.2.picks_ref, s32[8]{0:T(128)} %and_select_fusion.2.sources_ref, bf16[256,32,128]{2,1,0:T(8,128)(2,1)} %bitcast.53, bf16[256,128,128]{2,1,0:T(8,128)(2,1)} %refs_47_.1, bf16[256,128,128]{2,1,0:T(8,128)(2,1)} %refs_47_.1, ...), custom_call_target="tpu_custom_call" | custom-call | flops 4026531840 | bytes 15728640 | tf_op jit(solution)/shard_map/pallas_call | solution.py:142
  88.4 7.0 %all-to-all-start = ((bf16[32,13,32,128]{3,2,1,0:T(8,128)(2,1)}), bf16[32,13,32,128]{3,2,1,0:T(8,128)(2,1)S(1)}, u32[]{:S(2)}, u32[]{:S(2)}) async-start(bf16[32,13,32,128]{3,2,1,0:T(8,128)(2,1)} %shard_map.68), calls=%async_computation | async-start | bytes 6815744 | tf_op jit(solution)/shard_map/all_to_all | solution.py:192
  95.5 72.3 %all-to-all-done = bf16[32,13,32,128]{3,2,1,0:T(8,128)(2,1)S(1)} async-done(((bf16[32,13,32,128]{3,2,1,0:T(8,128)(2,1)}), bf16[32,13,32,128]{3,2,1,0:T(8,128)(2,1)S(1)}, u32[]{:S(2)}, u32[]{:S(2)}) %all-to-all-start) | async-done | bytes 3407904 | tf_op jit(solution)/shard_map/all_to_all | solution.py:192
  168.0 1.3 gather_fusion.2
  169.3 0.8 convert_element_type.45
  170.4 0.9 fusion.10
  171.3 0.7 fusion.13
  172.2 1.0 fusion
  (63 shorter events, 7.0 us)
Async XLA Ops:
  0.6 0.8 copy-start
  1.4 1.8 %copy-start.1 = (bf16[8,32,128]{2,1,0:T(8,128)(2,1)S(1)}, bf16[8,32,128]{2,1,0:T(8,128)(2,1)}, u32[]{:S(2)}) copy-start(bf16[8,32,128]{2,1,0:T(8,128)(2,1)} %param.5) | copy-start | bytes 196612
  3.4 5.5 %collective-permute-start = (bf16[8,4224]{1,0:T(8,128)(2,1)S(1)}, bf16[8,4224]{1,0:T(8,128)(2,1)S(1)}, u32[]{:S(2)}, u32[]{:S(2)}) collective-permute-start(bf16[8,4224]{1,0:T(8,128)(2,1)S(1)} %concatenate.6), channel_id=1, source_target_pairs={{0,1},{1,2},{2,3},{3,0},{4,5},{5,6},{6,7},{7,4},{8,9},{9,10},{10,1... | collective-permute-start | bytes 202760 | tf_op jit(solution)/shard_map/ppermute | solution.py:34
  5.0 4.8 %collective-permute-start.2 = (bf16[8,4224]{1,0:T(8,128)(2,1)S(1)}, bf16[8,4224]{1,0:T(8,128)(2,1)S(1)}, u32[]{:S(2)}, u32[]{:S(2)}) collective-permute-start(bf16[8,4224]{1,0:T(8,128)(2,1)S(1)} %concatenate.6), channel_id=1, source_target_pairs={{0,3},{1,0},{2,1},{3,2},{4,7},{5,4},{6,5},{7,6},{8,11},{9,8},{10,9... | collective-permute-start | bytes 202760 | tf_op jit(solution)/shard_map/ppermute | solution.py:34
  8.9 5.5 %collective-permute-start.1 = (bf16[8,4224]{1,0:T(8,128)(2,1)S(1)}, bf16[8,4224]{1,0:T(8,128)(2,1)S(1)}, u32[]{:S(2)}, u32[]{:S(2)}) collective-permute-start(bf16[8,4224]{1,0:T(8,128)(2,1)S(1)} %collective-permute-done), channel_id=1, source_target_pairs={{0,1},{1,2},{2,3},{3,0},{4,5},{5,6},{6,7},{7,4},{8,9},{9,10},{10,1... | collective-permute-start | bytes 202760 | tf_op jit(solution)/shard_map/ppermute | solution.py:34
  15.1 10.4 %collective-permute-start.3 = (bf16[4,8,4224]{2,1,0:T(8,128)(2,1)S(1)}, bf16[4,8,4224]{2,1,0:T(8,128)(2,1)S(1)}, u32[]{:S(2)}, u32[]{:S(2)}) collective-permute-start(bf16[4,8,4224]{2,1,0:T(8,128)(2,1)S(1)} %broadcast_select_fusion), channel_id=1, source_target_pairs={{0,4},{4,8},{8,12},{12,16},{16,20},{20,24},{24,28},{28,0},{1,5},{5... | collective-permute-start | bytes 811016 | tf_op jit(solution)/shard_map/ppermute | solution.py:34
  17.3 8.3 %collective-permute-start.7 = (bf16[4,8,4224]{2,1,0:T(8,128)(2,1)S(1)}, bf16[4,8,4224]{2,1,0:T(8,128)(2,1)S(1)}, u32[]{:S(2)}, u32[]{:S(2)}) collective-permute-start(bf16[4,8,4224]{2,1,0:T(8,128)(2,1)S(1)} %broadcast_select_fusion), channel_id=1, source_target_pairs={{0,28},{4,0},{8,4},{12,8},{16,12},{20,16},{24,20},{28,24},{1,29},{... | collective-permute-start | bytes 811016 | tf_op jit(solution)/shard_map/ppermute | solution.py:34
  25.5 8.3 %collective-permute-start.4 = (bf16[4,8,4224]{2,1,0:T(8,128)(2,1)S(1)}, bf16[4,8,4224]{2,1,0:T(8,128)(2,1)S(1)}, u32[]{:S(2)}, u32[]{:S(2)}) collective-permute-start(bf16[4,8,4224]{2,1,0:T(8,128)(2,1)S(1)} %collective-permute-done.3), channel_id=1, source_target_pairs={{0,4},{4,8},{8,12},{12,16},{16,20},{20,24},{24,28},{28,0},{1,5},{5... | collective-permute-start | bytes 811016 | tf_op jit(solution)/shard_map/ppermute | solution.py:34
  25.6 8.3 %collective-permute-start.8 = (bf16[4,8,4224]{2,1,0:T(8,128)(2,1)S(1)}, bf16[4,8,4224]{2,1,0:T(8,128)(2,1)S(1)}, u32[]{:S(2)}, u32[]{:S(2)}) collective-permute-start(bf16[4,8,4224]{2,1,0:T(8,128)(2,1)S(1)} %collective-permute-done.7), channel_id=1, source_target_pairs={{0,28},{4,0},{8,4},{12,8},{16,12},{20,16},{24,20},{28,24},{1,29},{... | collective-permute-start | bytes 811016 | tf_op jit(solution)/shard_map/ppermute | solution.py:34
  33.8 9.5 %collective-permute-start.5 = (bf16[4,8,4224]{2,1,0:T(8,128)(2,1)S(1)}, bf16[4,8,4224]{2,1,0:T(8,128)(2,1)S(1)}, u32[]{:S(2)}, u32[]{:S(2)}) collective-permute-start(bf16[4,8,4224]{2,1,0:T(8,128)(2,1)S(1)} %collective-permute-done.4), channel_id=1, source_target_pairs={{0,4},{4,8},{8,12},{12,16},{16,20},{20,24},{24,28},{28,0},{1,5},{5... | collective-permute-start | bytes 811016 | tf_op jit(solution)/shard_map/ppermute | solution.py:34
  33.8 17.1 %collective-permute-start.9 = (bf16[4,8,4224]{2,1,0:T(8,128)(2,1)S(1)}, bf16[4,8,4224]{2,1,0:T(8,128)(2,1)S(1)}, u32[]{:S(2)}, u32[]{:S(2)}) collective-permute-start(bf16[4,8,4224]{2,1,0:T(8,128)(2,1)S(1)} %collective-permute-done.8), channel_id=1, source_target_pairs={{0,28},{4,0},{8,4},{12,8},{16,12},{20,16},{24,20},{28,24},{1,29},{... | collective-permute-start | bytes 811016 | tf_op jit(solution)/shard_map/ppermute | solution.py:34
  43.3 7.7 %collective-permute-start.6 = (bf16[4,8,4224]{2,1,0:T(8,128)(2,1)S(1)}, bf16[4,8,4224]{2,1,0:T(8,128)(2,1)S(1)}, u32[]{:S(2)}, u32[]{:S(2)}) collective-permute-start(bf16[4,8,4224]{2,1,0:T(8,128)(2,1)S(1)} %collective-permute-done.5), channel_id=1, source_target_pairs={{0,4},{4,8},{8,12},{12,16},{16,20},{20,24},{24,28},{28,0},{1,5},{5... | collective-permute-start | bytes 811016 | tf_op jit(solution)/shard_map/ppermute | solution.py:34
  88.4 79.3 %all-to-all-start = ((bf16[32,13,32,128]{3,2,1,0:T(8,128)(2,1)}), bf16[32,13,32,128]{3,2,1,0:T(8,128)(2,1)S(1)}, u32[]{:S(2)}, u32[]{:S(2)}) async-start(bf16[32,13,32,128]{3,2,1,0:T(8,128)(2,1)} %shard_map.68), calls=%async_computation | async-start | bytes 6815744 | tf_op jit(solution)/shard_map/all_to_all | solution.py:192

commit v9 on v8

--- a/solution.py
+++ b/solution.py
@@ -120,7 +120,7 @@
             (1, tile_len, feature_dim), lambda s, sl, pk, sr: (sl[s * per * capacity + t], 0, 0)
         )
 
-    group = 2 if capacity % 2 == 0 else 1
+    group = 1
     grid_spec = pltpu.PrefetchScalarGridSpec(
         num_scalar_prefetch=3,
         grid=(steps,),

time: 175 us -> 176 us (level)
  no operation moved by 1% of the time
where the time goes in v9:
time: 176 us
  waiting for transfers between devices  101 us (57%)
  Pallas kernels  33.7 us (19%)
  starting transfers between devices  23.8 us (14%)
  local copies, waits for them, and re-layouts  7.94 us (5%)
  other arithmetic  6.78 us (4%)
    all_to_all x1, waiting for transfers between devices, body(): returned = lax.all_to_all(payload, BANK, 0, 0, tiled=True)  72.2 us
    pallas_call x1, Pallas kernels, holder_terms(): pl.pallas_call(functools.partial(holder_kernel, capacity, group, per), gr...  33.7 us
    ppermute x10, waiting for transfers between devices, shift(): return lax.ppermute(x, axis, [(i, (i + step) % size) for i in range(size)])  29.3 us
    ppermute x10, starting transfers between devices, shift(): return lax.ppermute(x, axis, [(i, (i + step) % size) for i in range(size)])  16.7 us
    all_to_all x1, starting transfers between devices, body(): returned = lax.all_to_all(payload, BANK, 0, 0, tiled=True)  7.07 us
  transfers between devices with their start and end apart: 11, of which 7 were waited for; matrix products, arithmetic and copies ran while one was open for 0% of the time, Pallas kernels for 0%

profile of v9, /device:TPU:4, one launch (start us, length us, event | category | flops | bytes accessed | tf_op | source)
XLA Modules:
  0.0 175.6 jit_solution(709704485997587484)
XLA Ops:
  0.6 0.7 compare_select_fusion
  1.5 1.1 gather_fusion
  3.4 1.6 collective-permute-start
  5.0 1.7 collective-permute-start.2
  6.7 2.2 %collective-permute-done = bf16[8,4224]{1,0:T(8,128)(2,1)S(1)} collective-permute-done((bf16[8,4224]{1,0:T(8,128)(2,1)S(1)}, bf16[8,4224]{1,0:T(8,128)(2,1)S(1)}, u32[]{:S(2)}, u32[]{:S(2)}) %collective-permute-start) | collective-permute-done | bytes 67616 | tf_op jit(solution)/shard_map/ppermute | solution.py:34
  9.8 4.6 %collective-permute-done.1 = bf16[8,4224]{1,0:T(8,128)(2,1)S(1)} collective-permute-done((bf16[8,4224]{1,0:T(8,128)(2,1)S(1)}, bf16[8,4224]{1,0:T(8,128)(2,1)S(1)}, u32[]{:S(2)}, u32[]{:S(2)}) %collective-permute-start.1) | collective-permute-done | bytes 67616 | tf_op jit(solution)/shard_map/ppermute | solution.py:34
  15.1 2.0 %collective-permute-start.3 = (bf16[4,8,4224]{2,1,0:T(8,128)(2,1)S(1)}, bf16[4,8,4224]{2,1,0:T(8,128)(2,1)S(1)}, u32[]{:S(2)}, u32[]{:S(2)}) collective-permute-start(bf16[4,8,4224]{2,1,0:T(8,128)(2,1)S(1)} %broadcast_select_fusion), channel_id=1, source_target_pairs={{0,4},{4,8},{8,12},{12,16},{16,20},{20,24},{24,28},{28,0},{1,5},{5... | collective-permute-start | bytes 811016 | tf_op jit(solution)/shard_map/ppermute | solution.py:34
  17.3 4.0 %collective-permute-start.7 = (bf16[4,8,4224]{2,1,0:T(8,128)(2,1)S(1)}, bf16[4,8,4224]{2,1,0:T(8,128)(2,1)S(1)}, u32[]{:S(2)}, u32[]{:S(2)}) collective-permute-start(bf16[4,8,4224]{2,1,0:T(8,128)(2,1)S(1)} %broadcast_select_fusion), channel_id=1, source_target_pairs={{0,28},{4,0},{8,4},{12,8},{16,12},{20,16},{24,20},{28,24},{1,29},{... | collective-permute-start | bytes 811016 | tf_op jit(solution)/shard_map/ppermute | solution.py:34
  21.3 4.2 %collective-permute-done.3 = bf16[4,8,4224]{2,1,0:T(8,128)(2,1)S(1)} collective-permute-done((bf16[4,8,4224]{2,1,0:T(8,128)(2,1)S(1)}, bf16[4,8,4224]{2,1,0:T(8,128)(2,1)S(1)}, u32[]{:S(2)}, u32[]{:S(2)}) %collective-permute-start.3) | collective-permute-done | bytes 270368 | tf_op jit(solution)/shard_map/ppermute | solution.py:34
  25.6 3.4 %collective-permute-start.8 = (bf16[4,8,4224]{2,1,0:T(8,128)(2,1)S(1)}, bf16[4,8,4224]{2,1,0:T(8,128)(2,1)S(1)}, u32[]{:S(2)}, u32[]{:S(2)}) collective-permute-start(bf16[4,8,4224]{2,1,0:T(8,128)(2,1)S(1)} %collective-permute-done.7), channel_id=1, source_target_pairs={{0,28},{4,0},{8,4},{12,8},{16,12},{20,16},{24,20},{28,24},{1,29},{... | collective-permute-start | bytes 811016 | tf_op jit(solution)/shard_map/ppermute | solution.py:34
  29.0 4.8 %collective-permute-done.4 = bf16[4,8,4224]{2,1,0:T(8,128)(2,1)S(1)} collective-permute-done((bf16[4,8,4224]{2,1,0:T(8,128)(2,1)S(1)}, bf16[4,8,4224]{2,1,0:T(8,128)(2,1)S(1)}, u32[]{:S(2)}, u32[]{:S(2)}) %collective-permute-start.4) | collective-permute-done | bytes 270368 | tf_op jit(solution)/shard_map/ppermute | solution.py:34
  33.8 3.7 %collective-permute-start.9 = (bf16[4,8,4224]{2,1,0:T(8,128)(2,1)S(1)}, bf16[4,8,4224]{2,1,0:T(8,128)(2,1)S(1)}, u32[]{:S(2)}, u32[]{:S(2)}) collective-permute-start(bf16[4,8,4224]{2,1,0:T(8,128)(2,1)S(1)} %collective-permute-done.8), channel_id=1, source_target_pairs={{0,28},{4,0},{8,4},{12,8},{16,12},{20,16},{24,20},{28,24},{1,29},{... | collective-permute-start | bytes 811016 | tf_op jit(solution)/shard_map/ppermute | solution.py:34
  37.5 5.7 %collective-permute-done.5 = bf16[4,8,4224]{2,1,0:T(8,128)(2,1)S(1)} collective-permute-done((bf16[4,8,4224]{2,1,0:T(8,128)(2,1)S(1)}, bf16[4,8,4224]{2,1,0:T(8,128)(2,1)S(1)}, u32[]{:S(2)}, u32[]{:S(2)}) %collective-permute-start.5) | collective-permute-done | bytes 270368 | tf_op jit(solution)/shard_map/ppermute | solution.py:34
  43.3 7.6 %collective-permute-done.6 = bf16[4,8,4224]{2,1,0:T(8,128)(2,1)S(1)} collective-permute-done((bf16[4,8,4224]{2,1,0:T(8,128)(2,1)S(1)}, bf16[4,8,4224]{2,1,0:T(8,128)(2,1)S(1)}, u32[]{:S(2)}, u32[]{:S(2)}) %collective-permute-start.6) | collective-permute-done | bytes 270368 | tf_op jit(solution)/shard_map/ppermute | solution.py:34
  51.4 1.9 %copy.16 = bf16[32,8,32,128]{3,2,1,0:T(8,128)(2,1)} copy(bf16[32,8,32,128]{3,1,2,0:T(8,128)(2,1)S(1)} %slice_bitcast_fusion) | data formatting | bytes 4194304
  55.2 0.7 reshape.317.slots_ref
  55.9 33.7 %shard_map.68 = bf16[32,13,32,128]{3,2,1,0:T(8,128)(2,1)} custom-call(s32[384]{0:T(512)} %reshape.317.slots_ref, s32[384]{0:T(512)} %add_select_fusion.2.picks_ref, s32[8]{0:T(128)} %and_select_fusion.2.sources_ref, bf16[256,32,128]{2,1,0:T(8,128)(2,1)} %bitcast.53, bf16[256,128,128]{2,1,0:T(8,128)(2,1)} %refs_47_.1, bf16[256,128,128]{2,1,0:T(8,128)(2,1)} %refs_47_.1, ...), custom_call_target="tpu_custom_call" | custom-call | flops 3623878656 | bytes 15728640 | tf_op jit(solution)/shard_map/pallas_call | solution.py:142
  89.6 7.1 %all-to-all-start = ((bf16[32,13,32,128]{3,2,1,0:T(8,128)(2,1)}), bf16[32,13,32,128]{3,2,1,0:T(8,128)(2,1)S(1)}, u32[]{:S(2)}, u32[]{:S(2)}) async-start(bf16[32,13,32,128]{3,2,1,0:T(8,128)(2,1)} %shard_map.68), calls=%async_computation | async-start | bytes 6815744 | tf_op jit(solution)/shard_map/all_to_all | solution.py:192
  96.7 72.2 %all-to-all-done = bf16[32,13,32,128]{3,2,1,0:T(8,128)(2,1)S(1)} async-done(((bf16[32,13,32,128]{3,2,1,0:T(8,128)(2,1)}), bf16[32,13,32,128]{3,2,1,0:T(8,128)(2,1)S(1)}, u32[]{:S(2)}, u32[]{:S(2)}) %all-to-all-start) | async-done | bytes 3407904 | tf_op jit(solution)/shard_map/all_to_all | solution.py:192
  169.1 1.3 gather_fusion.2
  170.4 0.8 convert_element_type.45
  171.6 0.9 fusion.10
  172.4 0.7 fusion.13
  173.3 1.0 fusion
  (63 shorter events, 7.0 us)
Async XLA Ops:
  0.6 0.8 copy-start
  1.4 1.8 %copy-start.1 = (bf16[8,32,128]{2,1,0:T(8,128)(2,1)S(1)}, bf16[8,32,128]{2,1,0:T(8,128)(2,1)}, u32[]{:S(2)}) copy-start(bf16[8,32,128]{2,1,0:T(8,128)(2,1)} %param.5) | copy-start | bytes 196612
  3.4 5.5 %collective-permute-start = (bf16[8,4224]{1,0:T(8,128)(2,1)S(1)}, bf16[8,4224]{1,0:T(8,128)(2,1)S(1)}, u32[]{:S(2)}, u32[]{:S(2)}) collective-permute-start(bf16[8,4224]{1,0:T(8,128)(2,1)S(1)} %concatenate.6), channel_id=1, source_target_pairs={{0,1},{1,2},{2,3},{3,0},{4,5},{5,6},{6,7},{7,4},{8,9},{9,10},{10,1... | collective-permute-start | bytes 202760 | tf_op jit(solution)/shard_map/ppermute | solution.py:34
  5.0 4.8 %collective-permute-start.2 = (bf16[8,4224]{1,0:T(8,128)(2,1)S(1)}, bf16[8,4224]{1,0:T(8,128)(2,1)S(1)}, u32[]{:S(2)}, u32[]{:S(2)}) collective-permute-start(bf16[8,4224]{1,0:T(8,128)(2,1)S(1)} %concatenate.6), channel_id=1, source_target_pairs={{0,3},{1,0},{2,1},{3,2},{4,7},{5,4},{6,5},{7,6},{8,11},{9,8},{10,9... | collective-permute-start | bytes 202760 | tf_op jit(solution)/shard_map/ppermute | solution.py:34
  8.9 5.5 %collective-permute-start.1 = (bf16[8,4224]{1,0:T(8,128)(2,1)S(1)}, bf16[8,4224]{1,0:T(8,128)(2,1)S(1)}, u32[]{:S(2)}, u32[]{:S(2)}) collective-permute-start(bf16[8,4224]{1,0:T(8,128)(2,1)S(1)} %collective-permute-done), channel_id=1, source_target_pairs={{0,1},{1,2},{2,3},{3,0},{4,5},{5,6},{6,7},{7,4},{8,9},{9,10},{10,1... | collective-permute-start | bytes 202760 | tf_op jit(solution)/shard_map/ppermute | solution.py:34
  15.1 10.4 %collective-permute-start.3 = (bf16[4,8,4224]{2,1,0:T(8,128)(2,1)S(1)}, bf16[4,8,4224]{2,1,0:T(8,128)(2,1)S(1)}, u32[]{:S(2)}, u32[]{:S(2)}) collective-permute-start(bf16[4,8,4224]{2,1,0:T(8,128)(2,1)S(1)} %broadcast_select_fusion), channel_id=1, source_target_pairs={{0,4},{4,8},{8,12},{12,16},{16,20},{20,24},{24,28},{28,0},{1,5},{5... | collective-permute-start | bytes 811016 | tf_op jit(solution)/shard_map/ppermute | solution.py:34
  17.3 8.3 %collective-permute-start.7 = (bf16[4,8,4224]{2,1,0:T(8,128)(2,1)S(1)}, bf16[4,8,4224]{2,1,0:T(8,128)(2,1)S(1)}, u32[]{:S(2)}, u32[]{:S(2)}) collective-permute-start(bf16[4,8,4224]{2,1,0:T(8,128)(2,1)S(1)} %broadcast_select_fusion), channel_id=1, source_target_pairs={{0,28},{4,0},{8,4},{12,8},{16,12},{20,16},{24,20},{28,24},{1,29},{... | collective-permute-start | bytes 811016 | tf_op jit(solution)/shard_map/ppermute | solution.py:34
  25.5 8.3 %collective-permute-start.4 = (bf16[4,8,4224]{2,1,0:T(8,128)(2,1)S(1)}, bf16[4,8,4224]{2,1,0:T(8,128)(2,1)S(1)}, u32[]{:S(2)}, u32[]{:S(2)}) collective-permute-start(bf16[4,8,4224]{2,1,0:T(8,128)(2,1)S(1)} %collective-permute-done.3), channel_id=1, source_target_pairs={{0,4},{4,8},{8,12},{12,16},{16,20},{20,24},{24,28},{28,0},{1,5},{5... | collective-permute-start | bytes 811016 | tf_op jit(solution)/shard_map/ppermute | solution.py:34
  25.6 8.3 %collective-permute-start.8 = (bf16[4,8,4224]{2,1,0:T(8,128)(2,1)S(1)}, bf16[4,8,4224]{2,1,0:T(8,128)(2,1)S(1)}, u32[]{:S(2)}, u32[]{:S(2)}) collective-permute-start(bf16[4,8,4224]{2,1,0:T(8,128)(2,1)S(1)} %collective-permute-done.7), channel_id=1, source_target_pairs={{0,28},{4,0},{8,4},{12,8},{16,12},{20,16},{24,20},{28,24},{1,29},{... | collective-permute-start | bytes 811016 | tf_op jit(solution)/shard_map/ppermute | solution.py:34
  33.8 9.5 %collective-permute-start.5 = (bf16[4,8,4224]{2,1,0:T(8,128)(2,1)S(1)}, bf16[4,8,4224]{2,1,0:T(8,128)(2,1)S(1)}, u32[]{:S(2)}, u32[]{:S(2)}) collective-permute-start(bf16[4,8,4224]{2,1,0:T(8,128)(2,1)S(1)} %collective-permute-done.4), channel_id=1, source_target_pairs={{0,4},{4,8},{8,12},{12,16},{16,20},{20,24},{24,28},{28,0},{1,5},{5... | collective-permute-start | bytes 811016 | tf_op jit(solution)/shard_map/ppermute | solution.py:34
  33.8 17.1 %collective-permute-start.9 = (bf16[4,8,4224]{2,1,0:T(8,128)(2,1)S(1)}, bf16[4,8,4224]{2,1,0:T(8,128)(2,1)S(1)}, u32[]{:S(2)}, u32[]{:S(2)}) collective-permute-start(bf16[4,8,4224]{2,1,0:T(8,128)(2,1)S(1)} %collective-permute-done.8), channel_id=1, source_target_pairs={{0,28},{4,0},{8,4},{12,8},{16,12},{20,16},{24,20},{28,24},{1,29},{... | collective-permute-start | bytes 811016 | tf_op jit(solution)/shard_map/ppermute | solution.py:34
  43.3 7.7 %collective-permute-start.6 = (bf16[4,8,4224]{2,1,0:T(8,128)(2,1)S(1)}, bf16[4,8,4224]{2,1,0:T(8,128)(2,1)S(1)}, u32[]{:S(2)}, u32[]{:S(2)}) collective-permute-start(bf16[4,8,4224]{2,1,0:T(8,128)(2,1)S(1)} %collective-permute-done.5), channel_id=1, source_target_pairs={{0,4},{4,8},{8,12},{12,16},{16,20},{20,24},{24,28},{28,0},{1,5},{5... | collective-permute-start | bytes 811016 | tf_op jit(solution)/shard_map/ppermute | solution.py:34
  89.6 79.3 %all-to-all-start = ((bf16[32,13,32,128]{3,2,1,0:T(8,128)(2,1)}), bf16[32,13,32,128]{3,2,1,0:T(8,128)(2,1)S(1)}, u32[]{:S(2)}, u32[]{:S(2)}) async-start(bf16[32,13,32,128]{3,2,1,0:T(8,128)(2,1)} %shard_map.68), calls=%async_computation | async-start | bytes 6815744 | tf_op jit(solution)/shard_map/all_to_all | solution.py:192

commit v10 on v9

--- a/solution.py
+++ b/solution.py
@@ -120,7 +120,7 @@
             (1, tile_len, feature_dim), lambda s, sl, pk, sr: (sl[s * per * capacity + t], 0, 0)
         )
 
-    group = 1
+    group = 3 if capacity % 3 == 0 else 1
     grid_spec = pltpu.PrefetchScalarGridSpec(
         num_scalar_prefetch=3,
         grid=(steps,),

time: 176 us -> 176 us (level)
  no operation moved by 1% of the time
where the time goes in v10:
time: 176 us
  waiting for transfers between devices  101 us (57%)
  Pallas kernels  33.8 us (19%)
  starting transfers between devices  23.9 us (14%)
  local copies, waits for them, and re-layouts  7.94 us (5%)
  other arithmetic  6.78 us (4%)
    all_to_all x1, waiting for transfers between devices, body(): returned = lax.all_to_all(payload, BANK, 0, 0, tiled=True)  72.2 us
    pallas_call x1, Pallas kernels, holder_terms(): pl.pallas_call(functools.partial(holder_kernel, capacity, group, per), gr...  33.8 us
    ppermute x10, waiting for transfers between devices, shift(): return lax.ppermute(x, axis, [(i, (i + step) % size) for i in range(size)])  29.3 us
    ppermute x10, starting transfers between devices, shift(): return lax.ppermute(x, axis, [(i, (i + step) % size) for i in range(size)])  16.7 us
    all_to_all x1, starting transfers between devices, body(): returned = lax.all_to_all(payload, BANK, 0, 0, tiled=True)  7.13 us
  transfers between devices with their start and end apart: 11, of which 7 were waited for; matrix products, arithmetic and copies ran while one was open for 0% of the time, Pallas kernels for 0%

profile of v10, /device:TPU:4, one launch (start us, length us, event | category | flops | bytes accessed | tf_op | source)
XLA Modules:
  0.0 175.7 jit_solution(13189477168835876164)
XLA Ops:
  0.6 0.7 compare_select_fusion
  1.5 1.1 gather_fusion
  3.4 1.6 collective-permute-start
  5.0 1.7 collective-permute-start.2
  6.7 2.2 %collective-permute-done = bf16[8,4224]{1,0:T(8,128)(2,1)S(1)} collective-permute-done((bf16[8,4224]{1,0:T(8,128)(2,1)S(1)}, bf16[8,4224]{1,0:T(8,128)(2,1)S(1)}, u32[]{:S(2)}, u32[]{:S(2)}) %collective-permute-start) | collective-permute-done | bytes 67616 | tf_op jit(solution)/shard_map/ppermute | solution.py:34
  9.8 4.6 %collective-permute-done.1 = bf16[8,4224]{1,0:T(8,128)(2,1)S(1)} collective-permute-done((bf16[8,4224]{1,0:T(8,128)(2,1)S(1)}, bf16[8,4224]{1,0:T(8,128)(2,1)S(1)}, u32[]{:S(2)}, u32[]{:S(2)}) %collective-permute-start.1) | collective-permute-done | bytes 67616 | tf_op jit(solution)/shard_map/ppermute | solution.py:34
  15.1 2.0 %collective-permute-start.3 = (bf16[4,8,4224]{2,1,0:T(8,128)(2,1)S(1)}, bf16[4,8,4224]{2,1,0:T(8,128)(2,1)S(1)}, u32[]{:S(2)}, u32[]{:S(2)}) collective-permute-start(bf16[4,8,4224]{2,1,0:T(8,128)(2,1)S(1)} %broadcast_select_fusion), channel_id=1, source_target_pairs={{0,4},{4,8},{8,12},{12,16},{16,20},{20,24},{24,28},{28,0},{1,5},{5... | collective-permute-start | bytes 811016 | tf_op jit(solution)/shard_map/ppermute | solution.py:34
  17.3 4.0 %collective-permute-start.7 = (bf16[4,8,4224]{2,1,0:T(8,128)(2,1)S(1)}, bf16[4,8,4224]{2,1,0:T(8,128)(2,1)S(1)}, u32[]{:S(2)}, u32[]{:S(2)}) collective-permute-start(bf16[4,8,4224]{2,1,0:T(8,128)(2,1)S(1)} %broadcast_select_fusion), channel_id=1, source_target_pairs={{0,28},{4,0},{8,4},{12,8},{16,12},{20,16},{24,20},{28,24},{1,29},{... | collective-permute-start | bytes 811016 | tf_op jit(solution)/shard_map/ppermute | solution.py:34
  21.3 4.2 %collective-permute-done.3 = bf16[4,8,4224]{2,1,0:T(8,128)(2,1)S(1)} collective-permute-done((bf16[4,8,4224]{2,1,0:T(8,128)(2,1)S(1)}, bf16[4,8,4224]{2,1,0:T(8,128)(2,1)S(1)}, u32[]{:S(2)}, u32[]{:S(2)}) %collective-permute-start.3) | collective-permute-done | bytes 270368 | tf_op jit(solution)/shard_map/ppermute | solution.py:34
  25.6 3.4 %collective-permute-start.8 = (bf16[4,8,4224]{2,1,0:T(8,128)(2,1)S(1)}, bf16[4,8,4224]{2,1,0:T(8,128)(2,1)S(1)}, u32[]{:S(2)}, u32[]{:S(2)}) collective-permute-start(bf16[4,8,4224]{2,1,0:T(8,128)(2,1)S(1)} %collective-permute-done.7), channel_id=1, source_target_pairs={{0,28},{4,0},{8,4},{12,8},{16,12},{20,16},{24,20},{28,24},{1,29},{... | collective-permute-start | bytes 811016 | tf_op jit(solution)/shard_map/ppermute | solution.py:34
  29.0 4.8 %collective-permute-done.4 = bf16[4,8,4224]{2,1,0:T(8,128)(2,1)S(1)} collective-permute-done((bf16[4,8,4224]{2,1,0:T(8,128)(2,1)S(1)}, bf16[4,8,4224]{2,1,0:T(8,128)(2,1)S(1)}, u32[]{:S(2)}, u32[]{:S(2)}) %collective-permute-start.4) | collective-permute-done | bytes 270368 | tf_op jit(solution)/shard_map/ppermute | solution.py:34
  33.8 3.7 %collective-permute-start.9 = (bf16[4,8,4224]{2,1,0:T(8,128)(2,1)S(1)}, bf16[4,8,4224]{2,1,0:T(8,128)(2,1)S(1)}, u32[]{:S(2)}, u32[]{:S(2)}) collective-permute-start(bf16[4,8,4224]{2,1,0:T(8,128)(2,1)S(1)} %collective-permute-done.8), channel_id=1, source_target_pairs={{0,28},{4,0},{8,4},{12,8},{16,12},{20,16},{24,20},{28,24},{1,29},{... | collective-permute-start | bytes 811016 | tf_op jit(solution)/shard_map/ppermute | solution.py:34
  37.5 5.7 %collective-permute-done.5 = bf16[4,8,4224]{2,1,0:T(8,128)(2,1)S(1)} collective-permute-done((bf16[4,8,4224]{2,1,0:T(8,128)(2,1)S(1)}, bf16[4,8,4224]{2,1,0:T(8,128)(2,1)S(1)}, u32[]{:S(2)}, u32[]{:S(2)}) %collective-permute-start.5) | collective-permute-done | bytes 270368 | tf_op jit(solution)/shard_map/ppermute | solution.py:34
  43.3 7.6 %collective-permute-done.6 = bf16[4,8,4224]{2,1,0:T(8,128)(2,1)S(1)} collective-permute-done((bf16[4,8,4224]{2,1,0:T(8,128)(2,1)S(1)}, bf16[4,8,4224]{2,1,0:T(8,128)(2,1)S(1)}, u32[]{:S(2)}, u32[]{:S(2)}) %collective-permute-start.6) | collective-permute-done | bytes 270368 | tf_op jit(solution)/shard_map/ppermute | solution.py:34
  51.4 1.9 %copy.16 = bf16[32,8,32,128]{3,2,1,0:T(8,128)(2,1)} copy(bf16[32,8,32,128]{3,1,2,0:T(8,128)(2,1)S(1)} %slice_bitcast_fusion) | data formatting | bytes 4194304
  55.2 0.7 reshape.317.slots_ref
  55.9 33.8 %shard_map.68 = bf16[32,13,32,128]{3,2,1,0:T(8,128)(2,1)} custom-call(s32[384]{0:T(512)} %reshape.317.slots_ref, s32[384]{0:T(512)} %add_select_fusion.2.picks_ref, s32[8]{0:T(128)} %and_select_fusion.2.sources_ref, bf16[256,32,128]{2,1,0:T(8,128)(2,1)} %bitcast.53, bf16[256,128,128]{2,1,0:T(8,128)(2,1)} %refs_47_.1, bf16[256,128,128]{2,1,0:T(8,128)(2,1)} %refs_47_.1, ...), custom_call_target="tpu_custom_call" | custom-call | flops 4429185024 | bytes 15728640 | tf_op jit(solution)/shard_map/pallas_call | solution.py:142
  89.7 7.1 %all-to-all-start = ((bf16[32,13,32,128]{3,2,1,0:T(8,128)(2,1)}), bf16[32,13,32,128]{3,2,1,0:T(8,128)(2,1)S(1)}, u32[]{:S(2)}, u32[]{:S(2)}) async-start(bf16[32,13,32,128]{3,2,1,0:T(8,128)(2,1)} %shard_map.68), calls=%async_computation | async-start | bytes 6815744 | tf_op jit(solution)/shard_map/all_to_all | solution.py:192
  96.9 72.2 %all-to-all-done = bf16[32,13,32,128]{3,2,1,0:T(8,128)(2,1)S(1)} async-done(((bf16[32,13,32,128]{3,2,1,0:T(8,128)(2,1)}), bf16[32,13,32,128]{3,2,1,0:T(8,128)(2,1)S(1)}, u32[]{:S(2)}, u32[]{:S(2)}) %all-to-all-start) | async-done | bytes 3407904 | tf_op jit(solution)/shard_map/all_to_all | solution.py:192
  169.3 1.3 gather_fusion.2
  170.6 0.8 convert_element_type.45
  171.8 0.9 fusion.10
  172.6 0.7 fusion.13
  173.5 1.0 fusion
  (63 shorter events, 7.0 us)
Async XLA Ops:
  0.6 0.8 copy-start
  1.4 1.8 %copy-start.1 = (bf16[8,32,128]{2,1,0:T(8,128)(2,1)S(1)}, bf16[8,32,128]{2,1,0:T(8,128)(2,1)}, u32[]{:S(2)}) copy-start(bf16[8,32,128]{2,1,0:T(8,128)(2,1)} %param.5) | copy-start | bytes 196612
  3.4 5.5 %collective-permute-start = (bf16[8,4224]{1,0:T(8,128)(2,1)S(1)}, bf16[8,4224]{1,0:T(8,128)(2,1)S(1)}, u32[]{:S(2)}, u32[]{:S(2)}) collective-permute-start(bf16[8,4224]{1,0:T(8,128)(2,1)S(1)} %concatenate.6), channel_id=1, source_target_pairs={{0,1},{1,2},{2,3},{3,0},{4,5},{5,6},{6,7},{7,4},{8,9},{9,10},{10,1... | collective-permute-start | bytes 202760 | tf_op jit(solution)/shard_map/ppermute | solution.py:34
  5.0 4.8 %collective-permute-start.2 = (bf16[8,4224]{1,0:T(8,128)(2,1)S(1)}, bf16[8,4224]{1,0:T(8,128)(2,1)S(1)}, u32[]{:S(2)}, u32[]{:S(2)}) collective-permute-start(bf16[8,4224]{1,0:T(8,128)(2,1)S(1)} %concatenate.6), channel_id=1, source_target_pairs={{0,3},{1,0},{2,1},{3,2},{4,7},{5,4},{6,5},{7,6},{8,11},{9,8},{10,9... | collective-permute-start | bytes 202760 | tf_op jit(solution)/shard_map/ppermute | solution.py:34
  8.9 5.5 %collective-permute-start.1 = (bf16[8,4224]{1,0:T(8,128)(2,1)S(1)}, bf16[8,4224]{1,0:T(8,128)(2,1)S(1)}, u32[]{:S(2)}, u32[]{:S(2)}) collective-permute-start(bf16[8,4224]{1,0:T(8,128)(2,1)S(1)} %collective-permute-done), channel_id=1, source_target_pairs={{0,1},{1,2},{2,3},{3,0},{4,5},{5,6},{6,7},{7,4},{8,9},{9,10},{10,1... | collective-permute-start | bytes 202760 | tf_op jit(solution)/shard_map/ppermute | solution.py:34
  15.1 10.4 %collective-permute-start.3 = (bf16[4,8,4224]{2,1,0:T(8,128)(2,1)S(1)}, bf16[4,8,4224]{2,1,0:T(8,128)(2,1)S(1)}, u32[]{:S(2)}, u32[]{:S(2)}) collective-permute-start(bf16[4,8,4224]{2,1,0:T(8,128)(2,1)S(1)} %broadcast_select_fusion), channel_id=1, source_target_pairs={{0,4},{4,8},{8,12},{12,16},{16,20},{20,24},{24,28},{28,0},{1,5},{5... | collective-permute-start | bytes 811016 | tf_op jit(solution)/shard_map/ppermute | solution.py:34
  17.3 8.3 %collective-permute-start.7 = (bf16[4,8,4224]{2,1,0:T(8,128)(2,1)S(1)}, bf16[4,8,4224]{2,1,0:T(8,128)(2,1)S(1)}, u32[]{:S(2)}, u32[]{:S(2)}) collective-permute-start(bf16[4,8,4224]{2,1,0:T(8,128)(2,1)S(1)} %broadcast_select_fusion), channel_id=1, source_target_pairs={{0,28},{4,0},{8,4},{12,8},{16,12},{20,16},{24,20},{28,24},{1,29},{... | collective-permute-start | bytes 811016 | tf_op jit(solution)/shard_map/ppermute | solution.py:34
  25.5 8.3 %collective-permute-start.4 = (bf16[4,8,4224]{2,1,0:T(8,128)(2,1)S(1)}, bf16[4,8,4224]{2,1,0:T(8,128)(2,1)S(1)}, u32[]{:S(2)}, u32[]{:S(2)}) collective-permute-start(bf16[4,8,4224]{2,1,0:T(8,128)(2,1)S(1)} %collective-permute-done.3), channel_id=1, source_target_pairs={{0,4},{4,8},{8,12},{12,16},{16,20},{20,24},{24,28},{28,0},{1,5},{5... | collective-permute-start | bytes 811016 | tf_op jit(solution)/shard_map/ppermute | solution.py:34
  25.6 8.3 %collective-permute-start.8 = (bf16[4,8,4224]{2,1,0:T(8,128)(2,1)S(1)}, bf16[4,8,4224]{2,1,0:T(8,128)(2,1)S(1)}, u32[]{:S(2)}, u32[]{:S(2)}) collective-permute-start(bf16[4,8,4224]{2,1,0:T(8,128)(2,1)S(1)} %collective-permute-done.7), channel_id=1, source_target_pairs={{0,28},{4,0},{8,4},{12,8},{16,12},{20,16},{24,20},{28,24},{1,29},{... | collective-permute-start | bytes 811016 | tf_op jit(solution)/shard_map/ppermute | solution.py:34
  33.8 9.5 %collective-permute-start.5 = (bf16[4,8,4224]{2,1,0:T(8,128)(2,1)S(1)}, bf16[4,8,4224]{2,1,0:T(8,128)(2,1)S(1)}, u32[]{:S(2)}, u32[]{:S(2)}) collective-permute-start(bf16[4,8,4224]{2,1,0:T(8,128)(2,1)S(1)} %collective-permute-done.4), channel_id=1, source_target_pairs={{0,4},{4,8},{8,12},{12,16},{16,20},{20,24},{24,28},{28,0},{1,5},{5... | collective-permute-start | bytes 811016 | tf_op jit(solution)/shard_map/ppermute | solution.py:34
  33.8 17.1 %collective-permute-start.9 = (bf16[4,8,4224]{2,1,0:T(8,128)(2,1)S(1)}, bf16[4,8,4224]{2,1,0:T(8,128)(2,1)S(1)}, u32[]{:S(2)}, u32[]{:S(2)}) collective-permute-start(bf16[4,8,4224]{2,1,0:T(8,128)(2,1)S(1)} %collective-permute-done.8), channel_id=1, source_target_pairs={{0,28},{4,0},{8,4},{12,8},{16,12},{20,16},{24,20},{28,24},{1,29},{... | collective-permute-start | bytes 811016 | tf_op jit(solution)/shard_map/ppermute | solution.py:34
  43.3 7.7 %collective-permute-start.6 = (bf16[4,8,4224]{2,1,0:T(8,128)(2,1)S(1)}, bf16[4,8,4224]{2,1,0:T(8,128)(2,1)S(1)}, u32[]{:S(2)}, u32[]{:S(2)}) collective-permute-start(bf16[4,8,4224]{2,1,0:T(8,128)(2,1)S(1)} %collective-permute-done.5), channel_id=1, source_target_pairs={{0,4},{4,8},{8,12},{12,16},{16,20},{20,24},{24,28},{28,0},{1,5},{5... | collective-permute-start | bytes 811016 | tf_op jit(solution)/shard_map/ppermute | solution.py:34
  89.7 79.4 %all-to-all-start = ((bf16[32,13,32,128]{3,2,1,0:T(8,128)(2,1)}), bf16[32,13,32,128]{3,2,1,0:T(8,128)(2,1)S(1)}, u32[]{:S(2)}, u32[]{:S(2)}) async-start(bf16[32,13,32,128]{3,2,1,0:T(8,128)(2,1)} %shard_map.68), calls=%async_computation | async-start | bytes 6815744 | tf_op jit(solution)/shard_map/all_to_all | solution.py:192
